TPU v7x, 32 devices: a whole 2x2x4 slice. The times are simulated.
32 devices in a mesh: grp: 4 (over z), exp: 8 (over y, x, core).
Axes of the slice: x: 2, y: 2, z: 4, core: 2. Of those that a mesh axis runs over, the one named last changes fastest.
Arguments:
- cotangent: bfloat16 [4096, 1440], P(('grp', 'exp')), may hold values from -6 to 6
- hidden: bfloat16 [4096, 4, 1440], P(('grp', 'exp')), may hold values from -0.29882812 to 0.29882812
- gates: bfloat16 [4096, 4], P(('grp', 'exp')), may hold values from 0.049804688 to 1
- expert_ids: int32 [4096, 4], P(('grp', 'exp')), may hold values from 0 to 15, all different within a row; in each aligned block of 128 rows (0 to 127, 128 to 255, ...) at most 40 rows name the same one
- group_counts: int32 [4], P('grp'), may hold values from 146 to 1024, as said below
- w_down: bfloat16 [16, 1440, 1440], P('exp', 'grp'), may hold values from -0.15625 to 0.15625
Outputs:
- d_hidden: bfloat16 [4096, 4, 1440], P(('grp', 'exp'))
- d_gate: bfloat16 [4096, 4], P(('grp', 'exp'))
- d_weight: float32 [16, 1440, 1440], P('exp', 'grp')
Inputs may be any that keep to these rules, and one draw needn't show every extreme that they name: `expert_ids`: within the rows of one device no expert is named more than 40 times, and every expert is named somewhere. `group_counts`: some group has all 1024 slots live, and some group only 146.
All inputs are finite; a program needn't handle non-finite values.
Results may differ from a plain program's by a relative error of at most 0.015.
Values may be sent and summed in bfloat16 or wider, within the bound.
No kernel may reach another device: no remote copies, remote signals or barrier semaphores. Data moves between devices by JAX's collectives and lax.ppermute only.
A program may use at most 128 MiB of HBM per device.

v0:
```python
import jax
import jax.numpy as jnp
from jax import lax
from jax.sharding import PartitionSpec as P

LOSS_SCALE = 32768


def body(cotangent, hidden, gates, expert_ids, group_counts, w_down):
    tok = cotangent.shape[0]
    top = expert_ids.shape[1]
    ffw = hidden.shape[2]
    width = cotangent.shape[1]
    n_exp = lax.axis_size("exp")
    exp_dev = w_down.shape[0]
    experts = exp_dev * n_exp
    most = 5 * tok * top // (4 * experts)
    count = group_counts[0]
    first_row = lax.axis_index("exp") * tok
    live = (first_row + jnp.arange(tok, dtype=jnp.int32) < count).astype(jnp.float32)
    total = lax.psum(count.astype(jnp.float32), "grp")
    scale = LOSS_SCALE / total
    weighted = (gates.astype(jnp.float32) * live[:, None]).astype(jnp.bfloat16)
    flat_ids = expert_ids.reshape(-1)
    onehot = (flat_ids[:, None] == jnp.arange(experts, dtype=jnp.int32)[None, :]).astype(jnp.int32)
    rank = jnp.sum((jnp.cumsum(onehot, axis=0) - onehot) * onehot, axis=1)
    target = flat_ids * most + rank
    slot_tok = jnp.arange(tok * top, dtype=jnp.int32) // top
    dy_buf = jnp.zeros((experts * most, width), jnp.bfloat16).at[target].set(cotangent[slot_tok])
    hid_buf = jnp.zeros((experts * most, ffw), jnp.bfloat16).at[target].set(hidden.reshape(-1, ffw))
    gate_buf = jnp.zeros((experts * most,), jnp.bfloat16).at[target].set(weighted.reshape(-1))
    dy_buf = dy_buf.reshape(n_exp, exp_dev * most, width)
    hid_buf = hid_buf.reshape(n_exp, exp_dev * most, ffw)
    gate_buf = gate_buf.reshape(n_exp, exp_dev * most)
    dy_recv, gate_recv = (
        lax.all_to_all(dy_buf, "exp", split_axis=0, concat_axis=0, tiled=True),
        lax.all_to_all(gate_buf, "exp", split_axis=0, concat_axis=0, tiled=True),
    )
    hid_recv = lax.all_to_all(hid_buf, "exp", split_axis=0, concat_axis=0, tiled=True)
    dy_four = dy_recv.reshape(n_exp, exp_dev, most, width)
    hid_four = hid_recv.reshape(n_exp, exp_dev, most, ffw)
    gate_three = gate_recv.reshape(n_exp, exp_dev, most).astype(jnp.float32)
    proj = jnp.einsum(
        "sjmd,jfd->sjmf",
        dy_four,
        lax.all_gather(w_down, "grp", axis=1, tiled=True),
        preferred_element_type=jnp.float32,
    )
    dh_rows = (gate_three[..., None] * proj).astype(jnp.bfloat16)
    inner = jnp.sum(hid_four.astype(jnp.float32) * proj, axis=3).astype(jnp.bfloat16)
    scaled = (gate_three[..., None] * dy_four.astype(jnp.float32)).astype(jnp.bfloat16)
    partial_grad = (
        jnp.einsum("sjmf,sjmd->jfd", hid_four, scaled, preferred_element_type=jnp.float32) * scale
    )
    d_weight = lax.psum_scatter(
        partial_grad.astype(jnp.bfloat16), "grp", scatter_dimension=1, tiled=True
    ).astype(jnp.float32)
    back_dh, back_inner = (
        lax.all_to_all(
            dh_rows.reshape(n_exp, exp_dev * most, ffw),
            "exp",
            split_axis=0,
            concat_axis=0,
            tiled=True,
        ),
        lax.all_to_all(
            inner.reshape(n_exp, exp_dev * most), "exp", split_axis=0, concat_axis=0, tiled=True
        ),
    )
    d_hidden = back_dh.reshape(experts * most, ffw)[target].reshape(tok, top, ffw)
    inner_tok = back_inner.reshape(-1)[target].reshape(tok, top)
    d_gate = (inner_tok.astype(jnp.float32) * live[:, None]).astype(jnp.bfloat16)
    return (d_hidden, d_gate, d_weight)


def solution(mesh):
    in_specs = (
        P(("grp", "exp"), None),
        P(("grp", "exp"), None, None),
        P(("grp", "exp"), None),
        P(("grp", "exp"), None),
        P("grp"),
        P("exp", "grp", None),
    )
    out_specs = (P(("grp", "exp"), None, None), P(("grp", "exp"), None), P("exp", "grp", None))
    return jax.shard_map(body, mesh=mesh, in_specs=in_specs, out_specs=out_specs, check_vma=False)
```

profile of v0, /device:TPU:2, one launch (start us, length us, event | category | flops | bytes accessed | tf_op | source)
XLA Modules:
  0.0 500.1 jit_solution(16202728035999669125)
XLA Ops:
  7.2 0.0 copy-start.3
  7.2 0.0 copy-start.4
  7.2 0.0 copy-start.1
  7.2 0.0 all-gather.2.cloned.1.call-start
  7.2 0.7 all-gather.2.cloned.1.call-update
  7.9 0.0 copy-done.3
  7.9 0.1 copy.45
  8.1 0.1 eq.25
  8.2 0.1 eq.29
  8.3 0.1 copy.44
  8.4 0.1 mul.61
  8.5 1.2 reduce-window.6
  9.7 0.2 slice_reduce_fusion
  10.6 0.0 copy-done.4
  10.6 0.1 copy.49
  10.8 0.1 reshape.204
  10.9 0.1 fusion.14
  11.0 3.8 scatter_custom_fusion
  14.8 0.7 all_to_all.25
  15.5 4.3 all-to-all-start
  19.7 0.0 copy-done.1
  19.7 1.6 copy.55
  21.3 0.8 reshape.220
  22.1 4.5 scatter_custom_fusion.2
  26.5 0.0 all-to-all-done
  26.5 0.0 copy-start.2
  26.5 4.3 all-to-all-start.3
  30.9 0.0 copy-done.2
  30.9 0.2 copy.52
  31.1 9.6 %scatter_custom_fusion.1 = bf16[640,1440]{1,0:T(8,128)(2,1)} fusion(s32[512]{0:T(512)S(1)} %bitcast.59, bf16[128,1440]{1,0:T(8,128)(2,1)S(1)} %copy.52, s32[1024]{0:T(1024)S(1)} %pad_clamp_fusion.1, bf16[]{:T(256)} %constant.15.clone.1), kind=kCustom, calls=%fused_computation.18 | custom fusion | bytes 1843202 | tf_op jit(solution)/shard_map/scatter | solution.py:29
  40.7 13.9 %all-to-all-done.3 = bf16[8,80,1440]{2,1,0:T(8,128)(2,1)S(1)} async-done(((bf16[8,80,1440]{2,1,0:T(8,128)(2,1)}), bf16[8,80,1440]{2,1,0:T(8,128)(2,1)S(1)}, u32[]{:S(2)}, u32[]{:S(2)}) %all-to-all-start.3) | async-done | bytes 1843232 | tf_op jit(solution)/shard_map/all_to_all | solution.py:39
  54.6 5.7 %all-to-all-start.1 = ((bf16[8,80,1440]{2,1,0:T(8,128)(2,1)}), bf16[8,80,1440]{2,1,0:T(8,128)(2,1)}, u32[]{:S(2)}, u32[]{:S(2)}) async-start(bf16[8,80,1440]{2,1,0:T(8,128)(2,1)} %bitcast.5), calls=%async_computation.1 | async-start | bytes 3932160 | tf_op jit(solution)/shard_map/all_to_all | solution.py:36
  60.3 0.0 all-reduce.3.cloned.1.call-start
  60.3 15.1 %psum.7 = f32[]{:T(128)} all-reduce(f32[]{:T(128)S(6)} %convert_element_type.90), channel_id=1, replica_groups=mesh['grp'=4,'exp'=8] {'grp'}, use_global_device_ids=true, to_apply=%region_7.8 | all-reduce | flops 1 | bytes 8 | tf_op jit(solution)/shard_map/psum | solution.py:21
  76.2 0.1 reshape.174
  76.2 8.0 %all-to-all-done.1 = bf16[8,80,1440]{2,1,0:T(8,128)(2,1)} async-done(((bf16[8,80,1440]{2,1,0:T(8,128)(2,1)}), bf16[8,80,1440]{2,1,0:T(8,128)(2,1)}, u32[]{:S(2)}, u32[]{:S(2)}) %all-to-all-start.1) | async-done | bytes 1843232 | tf_op jit(solution)/shard_map/all_to_all | solution.py:36
  84.2 84.0 %all-gather.2.cloned.1.call-done = bf16[2,1440,1440]{2,1,0:T(8,128)(2,1)} async-done(((bf16[2,360,1440]{2,1,0:T(8,128)(2,1)}), bf16[2,1440,1440]{2,1,0:T(8,128)(2,1)}) %all-gather.2.cloned.1.call-update) | async-done | bytes 8294416 | tf_op jit(solution)/shard_map/all_gather | solution.py:46
  168.2 9.6 %fusion.4 = (bf16[8,2,40]{2,0,1:T(8,128)(2,1)S(1)}, bf16[8,2,40,1440]{3,2,0,1:T(8,128)(2,1)}, bf16[8,2,40,1440]{3,2,0,1:T(8,128)(2,1)S(1)}) fusion(bf16[8,2,40,1440]{3,2,1,0:T(8,128)(2,1)S(1)} %bitcast.55, f32[8,2,40]{2,0,1:T(8,128)S(1)} %copy.51, bf16[8,2,40,1440]{3,2,1,0:T(8,128)(2,1)} %bitcast.6, bf16[2,1440,1440]{2,1,0:T(8,128)(2,1)} %all-gather.2.cloned.1.call-done), kind=kOutput, calls=%fused_computation.13 | convolution fusion | flops 2661580288 | bytes 15671040 | tf_op jit(solution)/shard_map/sjmd,jfd->sjmf/dot_general | solution.py:43
  177.8 7.1 %fusion = bf16[2,1440,1440]{2,1,0:T(8,128)(2,1)} fusion(bf16[8,2,40,1440]{3,2,1,0:T(8,128)(2,1)S(1)} %bitcast.56, f32[]{:T(128)S(6)} %div.13, bf16[8,2,40,1440]{3,2,0,1:T(8,128)(2,1)S(1)} %get-tuple-element.17), kind=kOutput, calls=%fused_computation.7 | convolution fusion | flops 2662502400 | bytes 11980804 | tf_op jit(solution)/shard_map/sjmf,sjmd->jfd/dot_general | solution.py:53
  184.8 0.0 copy-start
  184.8 0.0 all-reduce.3.cloned.1.call-update
  184.9 0.7 convert_element_type.95
  185.6 4.2 all-to-all-start.4
  189.8 0.0 copy-done
  189.8 1.5 copy.54
  191.2 1.7 all-to-all-done.4
  192.9 0.0 copy-start.5
  192.9 5.1 %all-to-all-start.2 = ((bf16[8,80,1440]{2,1,0:T(8,128)(2,1)}), bf16[8,80,1440]{2,1,0:T(8,128)(2,1)S(1)}, u32[]{:S(2)}, u32[]{:S(2)}) async-start(bf16[8,80,1440]{2,1,0:T(8,128)(2,1)} %bitcast.54), calls=%async_computation.2 | async-start | bytes 3932160 | tf_op jit(solution)/shard_map/all_to_all | solution.py:59
  198.0 0.0 copy-done.5
  198.0 0.6 dynamic-slice
  199.3 0.1 reshape.173
  199.4 3.5 gather_fusion.1
  202.9 0.1 reshape.175
  203.0 0.1 multiply_convert_fusion.1
  203.1 0.7 copy.62
  203.7 18.0 %all-to-all-done.2 = bf16[8,80,1440]{2,1,0:T(8,128)(2,1)S(1)} async-done(((bf16[8,80,1440]{2,1,0:T(8,128)(2,1)}), bf16[8,80,1440]{2,1,0:T(8,128)(2,1)S(1)}, u32[]{:S(2)}, u32[]{:S(2)}) %all-to-all-start.2) | async-done | bytes 1843232 | tf_op jit(solution)/shard_map/all_to_all | solution.py:59
  221.7 2.1 gather_fusion
  223.9 0.4 reshape.169
  224.3 2.4 copy.61
  226.7 262.2 %all-reduce.3.cloned.1.call-done = bf16[2,1440,1440]{2,1,0:T(8,128)(2,1)} async-done(((bf16[2,1440,1440]{2,1,0:T(8,128)(2,1)}), bf16[2,1440,1440]{2,1,0:T(8,128)(2,1)}) %all-reduce.3.cloned.1.call-update) | async-done | bytes 8294416
  488.9 4.3 dynamic-slice_convert_fusion
  (14 shorter events, 0.1 us)
Async XLA Ops:
  7.2 0.8 copy-start.3
  7.2 3.4 copy-start.4
  7.2 12.5 %copy-start.1 = (bf16[128,4,1440]{0,2,1:T(8,128)(2,1)S(1)}, bf16[128,4,1440]{0,2,1:T(8,128)(2,1)}, u32[]{:S(2)}) copy-start(bf16[128,4,1440]{0,2,1:T(8,128)(2,1)} %param.7) | copy-start | bytes 4423684
  7.2 161.0 %all-gather.2.cloned.1.call-start = ((), (), s32[]{:S(2)}) async-start(), calls=%async_computation.5 | async-start | bytes 11059200 | tf_op jit(solution)/shard_map/all_gather | solution.py:46
  15.5 11.1 %all-to-all-start = ((bf16[8,1,80]{2,1,0:T(2,128)(2,1)}), bf16[8,1,80]{2,1,0:T(2,128)(2,1)S(1)}, u32[]{:S(2)}, u32[]{:S(2)}) async-start(bf16[8,1,80]{2,1,0:T(2,128)(2,1)} %all_to_all.25), calls=%async_computation | async-start | bytes 8192 | tf_op jit(solution)/shard_map/all_to_all | solution.py:37
  26.5 4.3 copy-start.2
  26.5 28.1 %all-to-all-start.3 = ((bf16[8,80,1440]{2,1,0:T(8,128)(2,1)}), bf16[8,80,1440]{2,1,0:T(8,128)(2,1)S(1)}, u32[]{:S(2)}, u32[]{:S(2)}) async-start(bf16[8,80,1440]{2,1,0:T(8,128)(2,1)} %bitcast.12), calls=%async_computation.3 | async-start | bytes 3932160 | tf_op jit(solution)/shard_map/all_to_all | solution.py:39
  54.6 29.6 %all-to-all-start.1 = ((bf16[8,80,1440]{2,1,0:T(8,128)(2,1)}), bf16[8,80,1440]{2,1,0:T(8,128)(2,1)}, u32[]{:S(2)}, u32[]{:S(2)}) async-start(bf16[8,80,1440]{2,1,0:T(8,128)(2,1)} %bitcast.5), calls=%async_computation.1 | async-start | bytes 3932160 | tf_op jit(solution)/shard_map/all_to_all | solution.py:36
  60.3 428.6 %all-reduce.3.cloned.1.call-start = ((), (), s32[]{:S(2)}) async-start(), calls=%async_computation.6 | async-start | bytes 17694720
  184.8 4.9 copy-start
  185.6 7.3 %all-to-all-start.4 = ((bf16[8,1,80]{2,1,0:T(2,128)(2,1)}), bf16[8,1,80]{2,1,0:T(2,128)(2,1)S(1)}, u32[]{:S(2)}, u32[]{:S(2)}) async-start(bf16[8,1,80]{2,1,0:T(2,128)(2,1)} %convert_element_type.95), calls=%async_computation.4 | async-start | bytes 8192 | tf_op jit(solution)/shard_map/all_to_all | solution.py:66
  192.9 5.1 %copy-start.5 = (u32[32]{0:T(128)S(1)}, u32[32]{0:T(128)}, u32[]{:S(2)}) copy-start(u32[32]{0:T(128)} %constant.46) | copy-start | bytes 388
  192.9 28.9 %all-to-all-start.2 = ((bf16[8,80,1440]{2,1,0:T(8,128)(2,1)}), bf16[8,80,1440]{2,1,0:T(8,128)(2,1)S(1)}, u32[]{:S(2)}, u32[]{:S(2)}) async-start(bf16[8,80,1440]{2,1,0:T(8,128)(2,1)} %bitcast.54), calls=%async_computation.2 | async-start | bytes 3932160 | tf_op jit(solution)/shard_map/all_to_all | solution.py:59
Sparse Core Ops, SparseCore 0:
  9.6 158.5 all-gather.1
  185.0 303.8 all-reduce.2
where the time goes:
time: 502 us; the launch traced here: 500 us
  waiting for transfers between devices  388 us (77%)
  local copies, waits for them, and re-layouts  34.2 us (7%)
  starting transfers between devices  23.7 us (5%)
  matrix products  16.6 us (3%)
  between operations  16.3 us (3%)
  blocking collectives  15.1 us (3%)
  other arithmetic  5.77 us (1%)
    unnamed x3, waiting for transfers between devices  263 us
    all_gather x1, waiting for transfers between devices, body(): lax.all_gather(w_down, 'grp', axis=1, tiled=True)  84 us
    all_to_all x1, waiting for transfers between devices, body(): lax.all_to_all(dh_rows.reshape(n_exp, exp_dev * most, ffw), 'exp', split_...  18 us
    psum x1, blocking collectives, body(): total = lax.psum(count.astype(jnp.float32), 'grp')  15.1 us
    all_to_all x1, waiting for transfers between devices, body(): lax.all_to_all(hid_buf, 'exp', split_axis=0, concat_axis=0, tiled=True)  13.9 us
  transfers between devices with their start and end apart: 7, of which 6 were waited for; matrix products, arithmetic and copies ran while one was open for 7% of the time, Pallas kernels for 0%

commit v1 on v0

--- a/solution.py
+++ b/solution.py
@@ -12,13 +12,14 @@
     ffw = hidden.shape[2]
     width = cotangent.shape[1]
     n_exp = lax.axis_size("exp")
+    n_grp = lax.axis_size("grp")
     exp_dev = w_down.shape[0]
     experts = exp_dev * n_exp
     most = 5 * tok * top // (4 * experts)
     count = group_counts[0]
     first_row = lax.axis_index("exp") * tok
     live = (first_row + jnp.arange(tok, dtype=jnp.int32) < count).astype(jnp.float32)
-    total = lax.psum(count.astype(jnp.float32), "grp")
+    total = jnp.sum(lax.all_gather(group_counts, "grp", tiled=True).astype(jnp.float32))
     scale = LOSS_SCALE / total
     weighted = (gates.astype(jnp.float32) * live[:, None]).astype(jnp.bfloat16)
     flat_ids = expert_ids.reshape(-1)
@@ -50,11 +51,20 @@
     inner = jnp.sum(hid_four.astype(jnp.float32) * proj, axis=3).astype(jnp.bfloat16)
     scaled = (gate_three[..., None] * dy_four.astype(jnp.float32)).astype(jnp.bfloat16)
     partial_grad = (
-        jnp.einsum("sjmf,sjmd->jfd", hid_four, scaled, preferred_element_type=jnp.float32) * scale
+        jnp.einsum(
+            "sjmgf,sjmd->gjfd",
+            hid_four.reshape(n_exp, exp_dev, most, n_grp, ffw // n_grp),
+            scaled,
+            preferred_element_type=jnp.float32,
+        )
+        * scale
     )
-    d_weight = lax.psum_scatter(
-        partial_grad.astype(jnp.bfloat16), "grp", scatter_dimension=1, tiled=True
-    ).astype(jnp.float32)
+    grad_rows = partial_grad.astype(jnp.bfloat16).reshape(ffw * exp_dev, width)
+    d_weight = (
+        lax.psum_scatter(grad_rows, "grp", scatter_dimension=0, tiled=True)
+        .reshape(exp_dev, ffw // n_grp, width)
+        .astype(jnp.float32)
+    )
     back_dh, back_inner = (
         lax.all_to_all(
             dh_rows.reshape(n_exp, exp_dev * most, ffw),

time: 502 us -> 334 us (0.67)
  waiting for transfers between devices: 388 us -> 211 us
  local copies, waits for them, and re-layouts: 34.2 us -> 47.4 us
  blocking collectives: 15.1 us -> 8.62 us
    unnamed x3 -> x2, waiting for transfers between devices: 263 us -> 0.7 us
    reduce_scatter x0 -> x1, waiting for transfers between devices: none -> 102 us  [body(): lax.psum_scatter(grad_rows, 'grp', scatter_dimension=0, tiled=True)]
    all_gather x1, waiting for transfers between devices: 84 us -> 65.4 us  [body(): lax.all_gather(w_down, 'grp', axis=1, tiled=True)]
    psum x1 -> x0, blocking collectives: 15.1 us -> none  [body(): total = lax.psum(count.astype(jnp.float32), 'grp')]
    unnamed x0 -> x1, blocking collectives: none -> 8.62 us
    convert_element_type x0 -> x1, local copies, waits for them, and re-layouts: none -> 7.84 us  [body(): grad_rows = partial_grad.astype(jnp.bfloat16).reshape(ffw * exp_dev, width)]
  transfers between devices with their start and end apart: 7 -> 7, of which waited for: 6 -> 6; matrix products, arithmetic and copies ran while one was open for 7% -> 21% of each run, Pallas kernels for 0% -> 0%
where the time goes in v1:
time: 334 us; the launch traced here: 332 us
  waiting for transfers between devices  211 us (63%)
  local copies, waits for them, and re-layouts  47.4 us (14%)
  starting transfers between devices  23.7 us (7%)
  matrix products  19.3 us (6%)
  between operations  15.6 us (5%)
  blocking collectives  8.62 us (3%)
  other arithmetic  6.37 us (2%)
    reduce_scatter x1, waiting for transfers between devices, body(): lax.psum_scatter(grad_rows, 'grp', scatter_dimension=0, tiled=True)  102 us
    all_gather x1, waiting for transfers between devices, body(): lax.all_gather(w_down, 'grp', axis=1, tiled=True)  65.4 us
    all_to_all x1, waiting for transfers between devices, body(): lax.all_to_all(dh_rows.reshape(n_exp, exp_dev * most, ffw), 'exp', split_...  19.3 us
    all_to_all x1, waiting for transfers between devices, body(): lax.all_to_all(hid_buf, 'exp', split_axis=0, concat_axis=0, tiled=True)  14 us
    dot_general x1, matrix products, body(): jnp.einsum('sjmgf,sjmd->gjfd', hid_four.reshape(n_exp, exp_dev, most, n_g...  10.5 us
    scatter x1, local copies, waits for them, and re-layouts, body(): jnp.zeros((experts * most, width), jnp.bfloat16).at[target]  9.55 us
    all_to_all x1, waiting for transfers between devices, body(): lax.all_to_all(dy_buf, 'exp', split_axis=0, concat_axis=0, tiled=True)  9.49 us
    dot_general x1, matrix products, body(): jnp.einsum('sjmd,jfd->sjmf', dy_four, lax.all_gather(w_down, 'grp', axis=...  8.73 us
  transfers between devices with their start and end apart: 7, of which 6 were waited for; matrix products, arithmetic and copies ran while one was open for 21% of the time, Pallas kernels for 0%

profile of v1, /device:TPU:2, one launch (start us, length us, event | category | flops | bytes accessed | tf_op | source)
XLA Modules:
  0.0 331.6 jit_solution(14407678769083824106)
XLA Ops:
  7.2 0.0 copy-start.2
  7.2 0.0 copy-start.3
  7.2 0.0 copy-start
  7.2 0.0 all-gather.2.cloned.1.call-start
  7.2 0.7 all-gather.2.cloned.1.call-update
  7.9 0.0 copy-done.2
  7.9 0.1 copy.47
  8.1 0.1 eq.29
  8.2 0.1 eq.25
  8.9 0.0 copy-done.3
  9.0 0.1 copy.51
  9.1 0.1 reshape.212
  9.2 0.1 copy.46
  9.3 0.1 mul.62
  9.5 1.2 reduce-window.6
  10.6 0.2 slice_reduce_fusion
  10.9 0.1 fusion.19
  11.0 3.8 %scatter_custom_fusion = bf16[640]{0:T(1024)(128)(2,1)S(1)} fusion(s32[512]{0:T(512)S(1)} %bitcast.73, bf16[512]{0:T(512)(128)(2,1)S(1)} %reshape.212, bf16[]{:T(256)} %constant.15.clone.1), kind=kCustom, calls=%fused_computation.48 | custom fusion | bytes 1282 | tf_op jit(solution)/shard_map/scatter | solution.py:32
  14.8 0.7 all_to_all.25
  15.5 4.3 %all-to-all-start = ((bf16[8,1,80]{2,1,0:T(2,128)(2,1)}), bf16[8,1,80]{2,1,0:T(2,128)(2,1)S(1)}, u32[]{:S(2)}, u32[]{:S(2)}) async-start(bf16[8,1,80]{2,1,0:T(2,128)(2,1)} %all_to_all.25), calls=%async_computation | async-start | bytes 8192 | tf_op jit(solution)/shard_map/all_to_all | solution.py:38
  19.7 0.0 copy-done
  19.7 1.6 copy.57
  21.3 0.8 reshape.228
  22.1 4.5 %scatter_custom_fusion.2 = bf16[640,1440]{1,0:T(8,128)(2,1)} fusion(s32[512]{0:T(512)S(1)} %bitcast.74, bf16[512,1440]{1,0:T(8,128)(2,1)S(1)} %reshape.228, bf16[]{:T(256)} %constant.15.clone.1), kind=kCustom, calls=%fused_computation.23 | custom fusion | bytes 1843202 | tf_op jit(solution)/shard_map/scatter | solution.py:31
  26.6 0.0 all-to-all-done
  26.6 0.0 copy-start.1
  26.6 4.3 %all-to-all-start.3 = ((bf16[8,80,1440]{2,1,0:T(8,128)(2,1)}), bf16[8,80,1440]{2,1,0:T(8,128)(2,1)S(1)}, u32[]{:S(2)}, u32[]{:S(2)}) async-start(bf16[8,80,1440]{2,1,0:T(8,128)(2,1)} %bitcast.71), calls=%async_computation.3 | async-start | bytes 3932160 | tf_op jit(solution)/shard_map/all_to_all | solution.py:40
  30.9 0.0 copy-done.1
  30.9 0.2 copy.54
  31.2 9.6 %scatter_custom_fusion.1 = bf16[640,1440]{1,0:T(8,128)(2,1)} fusion(s32[512]{0:T(512)S(1)} %bitcast.75, bf16[128,1440]{1,0:T(8,128)(2,1)S(1)} %copy.54, s32[1024]{0:T(1024)S(1)} %pad_clamp_fusion.1, bf16[]{:T(256)} %constant.15.clone.1), kind=kCustom, calls=%fused_computation.21 | custom fusion | bytes 1843202 | tf_op jit(solution)/shard_map/scatter | solution.py:30
  40.7 14.0 %all-to-all-done.3 = bf16[8,80,1440]{2,1,0:T(8,128)(2,1)S(1)} async-done(((bf16[8,80,1440]{2,1,0:T(8,128)(2,1)}), bf16[8,80,1440]{2,1,0:T(8,128)(2,1)S(1)}, u32[]{:S(2)}, u32[]{:S(2)}) %all-to-all-start.3) | async-done | bytes 1843232 | tf_op jit(solution)/shard_map/all_to_all | solution.py:40
  54.7 0.0 copy-start.4
  54.7 5.9 %all-to-all-start.1 = ((bf16[8,80,1440]{2,1,0:T(8,128)(2,1)}), bf16[8,80,1440]{2,1,0:T(8,128)(2,1)}, u32[]{:S(2)}, u32[]{:S(2)}) async-start(bf16[8,80,1440]{2,1,0:T(8,128)(2,1)} %bitcast.69), calls=%async_computation.1 | async-start | bytes 3932160 | tf_op jit(solution)/shard_map/all_to_all | solution.py:37
  60.5 0.0 reduce-scatter.2.cloned.1.call-start
  60.5 0.0 copy-done.4
  60.5 0.6 dynamic-slice
  61.1 0.8 dynamic-update-slice
  61.9 8.6 %all-reduce = s32[4]{0:T(128)S(1)} all-reduce(s32[4]{0:T(128)S(1)} %dynamic-update-slice), channel_id=1, replica_groups=mesh['grp'=4,'exp'=8] {'grp'}, use_global_device_ids=true, to_apply=%add | all-reduce | flops 4 | bytes 32
  70.5 0.6 convert_reduce_fusion.1
  71.8 0.1 reshape.180
  71.9 3.0 reshape_reshape.3
  74.9 9.5 %all-to-all-done.1 = bf16[8,80,1440]{2,1,0:T(8,128)(2,1)} async-done(((bf16[8,80,1440]{2,1,0:T(8,128)(2,1)}), bf16[8,80,1440]{2,1,0:T(8,128)(2,1)}, u32[]{:S(2)}, u32[]{:S(2)}) %all-to-all-start.1) | async-done | bytes 1843232 | tf_op jit(solution)/shard_map/all_to_all | solution.py:37
  84.4 10.5 %fusion.1 = bf16[4,2,360,1440]{3,2,0,1:T(8,128)(2,1)} fusion(f32[]{:T(128)S(6)} %div.13, bf16[8,2,40,4,360]{4,3,2,1,0:T(4,128)(2,1)} %reshape_reshape.3, f32[8,2,40]{2,0,1:T(8,128)S(1)} %copy.53, bf16[8,2,40,1440]{3,2,1,0:T(8,128)(2,1)} %bitcast.6), kind=kOutput, calls=%fused_computation.8 | convolution fusion | flops 2665267200 | bytes 11983364 | tf_op jit(solution)/shard_map/sjmgf,sjmd->gjfd/dot_general | solution.py:54
  94.9 7.8 %copy.63 = bf16[4,2,360,1440]{3,2,1,0:T(8,128)(2,1)} copy(bf16[4,2,360,1440]{3,2,0,1:T(8,128)(2,1)} %fusion.1) | data formatting | bytes 16588800 | tf_op jit(solution)/shard_map/convert_element_type | solution.py:62
  102.8 0.0 reduce-scatter.2.cloned.1.call-update
  102.8 65.4 %all-gather.2.cloned.1.call-done = bf16[2,1440,1440]{2,1,0:T(8,128)(2,1)} async-done(((bf16[2,360,1440]{2,1,0:T(8,128)(2,1)}), bf16[2,1440,1440]{2,1,0:T(8,128)(2,1)}) %all-gather.2.cloned.1.call-update) | async-done | bytes 8294416 | tf_op jit(solution)/shard_map/all_gather | solution.py:47
  168.2 8.7 %fusion.5 = (bf16[8,2,40]{2,0,1:T(8,128)(2,1)S(1)}, bf16[8,2,40,1440]{3,2,0,1:T(8,128)(2,1)}) fusion(f32[8,2,40]{2,0,1:T(8,128)S(1)} %copy.53, bf16[2,1440,1440]{2,1,0:T(8,128)(2,1)} %all-gather.2.cloned.1.call-done, bf16[8,2,40,1440]{3,2,1,0:T(8,128)(2,1)} %bitcast.6, bf16[8,2,40,1440]{3,2,1,0:T(8,128)(2,1)S(1)} %bitcast.68), kind=kOutput, calls=%fused_computation.14 | convolution fusion | flops 2658815488 | bytes 13827840 | tf_op jit(solution)/shard_map/sjmd,jfd->sjmf/dot_general | solution.py:44
  176.9 0.7 convert_element_type.109
  177.6 4.2 %all-to-all-start.4 = ((bf16[8,1,80]{2,1,0:T(2,128)(2,1)}), bf16[8,1,80]{2,1,0:T(2,128)(2,1)S(1)}, u32[]{:S(2)}, u32[]{:S(2)}) async-start(bf16[8,1,80]{2,1,0:T(2,128)(2,1)} %convert_element_type.109), calls=%async_computation.4 | async-start | bytes 8192 | tf_op jit(solution)/shard_map/all_to_all | solution.py:76
  181.8 3.0 copy.56
  184.8 0.1 all-to-all-done.4
  184.9 5.0 %all-to-all-start.2 = ((bf16[8,80,1440]{2,1,0:T(8,128)(2,1)}), bf16[8,80,1440]{2,1,0:T(8,128)(2,1)S(1)}, u32[]{:S(2)}, u32[]{:S(2)}) async-start(bf16[8,80,1440]{2,1,0:T(8,128)(2,1)} %bitcast.70), calls=%async_computation.2 | async-start | bytes 3932160 | tf_op jit(solution)/shard_map/all_to_all | solution.py:69
  189.9 0.1 reshape.178
  190.0 3.5 %gather_fusion.1 = bf16[512]{0:T(512)(128)(2,1)S(1)} fusion(bf16[640]{0:T(1024)(128)(2,1)S(1)} %reshape.178, s32[1024]{0:T(1024)S(1)} %pad_clamp_fusion), kind=kCustom, calls=%fused_computation.2 | custom fusion | bytes 4096 | tf_op jit(solution)/shard_map/gather | solution.py:81
  193.5 0.1 reshape.182
  193.6 0.1 multiply_convert_fusion.1
  193.7 0.7 copy.65
  194.4 19.3 %all-to-all-done.2 = bf16[8,80,1440]{2,1,0:T(8,128)(2,1)S(1)} async-done(((bf16[8,80,1440]{2,1,0:T(8,128)(2,1)}), bf16[8,80,1440]{2,1,0:T(8,128)(2,1)S(1)}, u32[]{:S(2)}, u32[]{:S(2)}) %all-to-all-start.2) | async-done | bytes 1843232 | tf_op jit(solution)/shard_map/all_to_all | solution.py:69
  213.6 2.1 gather_fusion
  215.8 0.4 reshape.175
  216.2 2.4 copy.64
  218.6 101.8 %reduce-scatter.2.cloned.1.call-done = bf16[720,1440]{1,0:T(8,128)(2,1)} async-done(((bf16[2880,1440]{1,0:T(8,128)(2,1)}), bf16[720,1440]{1,0:T(8,128)(2,1)}) %reduce-scatter.2.cloned.1.call-update) | async-done | bytes 2073616 | tf_op jit(solution)/shard_map/reduce_scatter | solution.py:64
  320.5 4.3 %convert.5 = f32[2,360,1440]{2,1,0:T(8,128)} convert(bf16[2,360,1440]{2,1,0:T(8,128)(2,1)} %bitcast.72) | non-fusion elementwise | flops 1036800 | bytes 6220800 | tf_op jit(solution)/shard_map/convert_element_type | solution.py:66
  (15 shorter events, 0.1 us)
Async XLA Ops:
  7.2 0.8 copy-start.2
  7.2 1.8 copy-start.3
  7.2 12.5 %copy-start = (bf16[128,4,1440]{0,2,1:T(8,128)(2,1)S(1)}, bf16[128,4,1440]{0,2,1:T(8,128)(2,1)}, u32[]{:S(2)}) copy-start(bf16[128,4,1440]{0,2,1:T(8,128)(2,1)} %param.7) | copy-start | bytes 4423684
  7.2 161.0 %all-gather.2.cloned.1.call-start = ((), (), s32[]{:S(2)}) async-start(), calls=%async_computation.6 | async-start | bytes 11059200 | tf_op jit(solution)/shard_map/all_gather | solution.py:47
  15.5 11.2 %all-to-all-start = ((bf16[8,1,80]{2,1,0:T(2,128)(2,1)}), bf16[8,1,80]{2,1,0:T(2,128)(2,1)S(1)}, u32[]{:S(2)}, u32[]{:S(2)}) async-start(bf16[8,1,80]{2,1,0:T(2,128)(2,1)} %all_to_all.25), calls=%async_computation | async-start | bytes 8192 | tf_op jit(solution)/shard_map/all_to_all | solution.py:38
  26.6 4.3 %copy-start.1 = (bf16[128,1440]{0,1:T(8,128)(2,1)S(1)}, bf16[128,1440]{0,1:T(8,128)(2,1)}, u32[]{:S(2)}) copy-start(bf16[128,1440]{0,1:T(8,128)(2,1)} %param.6) | copy-start | bytes 1105924
  26.6 28.1 %all-to-all-start.3 = ((bf16[8,80,1440]{2,1,0:T(8,128)(2,1)}), bf16[8,80,1440]{2,1,0:T(8,128)(2,1)S(1)}, u32[]{:S(2)}, u32[]{:S(2)}) async-start(bf16[8,80,1440]{2,1,0:T(8,128)(2,1)} %bitcast.71), calls=%async_computation.3 | async-start | bytes 3932160 | tf_op jit(solution)/shard_map/all_to_all | solution.py:40
  54.7 5.9 %copy-start.4 = (u32[32]{0:T(128)S(1)}, u32[32]{0:T(128)}, u32[]{:S(2)}) copy-start(u32[32]{0:T(128)} %constant.46) | copy-start | bytes 388
  54.7 29.7 %all-to-all-start.1 = ((bf16[8,80,1440]{2,1,0:T(8,128)(2,1)}), bf16[8,80,1440]{2,1,0:T(8,128)(2,1)}, u32[]{:S(2)}, u32[]{:S(2)}) async-start(bf16[8,80,1440]{2,1,0:T(8,128)(2,1)} %bitcast.69), calls=%async_computation.1 | async-start | bytes 3932160 | tf_op jit(solution)/shard_map/all_to_all | solution.py:37
  60.5 259.9 %reduce-scatter.2.cloned.1.call-start = ((), (), s32[]{:S(2)}) async-start(), calls=%async_computation.7 | async-start | bytes 11059200 | tf_op jit(solution)/shard_map/reduce_scatter | solution.py:64
  177.6 7.3 %all-to-all-start.4 = ((bf16[8,1,80]{2,1,0:T(2,128)(2,1)}), bf16[8,1,80]{2,1,0:T(2,128)(2,1)S(1)}, u32[]{:S(2)}, u32[]{:S(2)}) async-start(bf16[8,1,80]{2,1,0:T(2,128)(2,1)} %convert_element_type.109), calls=%async_computation.4 | async-start | bytes 8192 | tf_op jit(solution)/shard_map/all_to_all | solution.py:76
  184.9 28.7 %all-to-all-start.2 = ((bf16[8,80,1440]{2,1,0:T(8,128)(2,1)}), bf16[8,80,1440]{2,1,0:T(8,128)(2,1)S(1)}, u32[]{:S(2)}, u32[]{:S(2)}) async-start(bf16[8,80,1440]{2,1,0:T(8,128)(2,1)} %bitcast.70), calls=%async_computation.2 | async-start | bytes 3932160 | tf_op jit(solution)/shard_map/all_to_all | solution.py:69
Sparse Core Ops, SparseCore 0:
  9.6 158.5 all-gather.1
  170.5 149.8 reduce-scatter.1

commit v2 on v0

v2 whole, which is shorter than its diff:
```python
import jax
import jax.numpy as jnp
from jax import lax
from jax.sharding import PartitionSpec as P

LOSS_SCALE = 32768


def body(cotangent, hidden, gates, expert_ids, group_counts, w_down):
    tok, top = expert_ids.shape
    ffw = hidden.shape[2]
    width = cotangent.shape[1]
    n_exp = lax.axis_size("exp")
    n_grp = lax.axis_size("grp")
    exp_dev, f_loc = w_down.shape[0], w_down.shape[1]
    experts = exp_dev * n_exp
    most = 5 * tok * top // (4 * experts)
    slots = n_grp * tok * top
    rows = n_exp * n_grp * exp_dev * most

    counts = lax.all_gather(group_counts, "grp", tiled=True)
    count = group_counts[0]
    first_row = lax.axis_index("exp") * tok
    live = (first_row + jnp.arange(tok, dtype=jnp.int32) < count).astype(jnp.float32)
    total = jnp.sum(counts.astype(jnp.float32))
    scale = LOSS_SCALE / total
    weighted = (gates.astype(jnp.float32) * live[:, None]).astype(jnp.bfloat16)

    cot_all = lax.all_gather(cotangent, "grp", tiled=True)
    ids_all = lax.all_gather(expert_ids, "grp").reshape(n_grp, tok * top)
    wt_all = lax.all_gather(weighted, "grp").reshape(slots)
    hid_split = jnp.transpose(hidden.reshape(tok, top, n_grp, f_loc), (2, 0, 1, 3))
    hid_sl = lax.all_to_all(hid_split, "grp", split_axis=0, concat_axis=0, tiled=True)
    hid_sl = hid_sl.reshape(slots, f_loc)

    onehot = (ids_all[:, :, None] == jnp.arange(experts, dtype=jnp.int32)).astype(jnp.int32)
    rank = jnp.sum((jnp.cumsum(onehot, axis=1) - onehot) * onehot, axis=2)
    dest = ids_all // exp_dev
    src = jnp.arange(n_grp, dtype=jnp.int32)[:, None]
    target = (((dest * n_grp + src) * exp_dev + ids_all % exp_dev) * most + rank).reshape(slots)
    slot_ids = jnp.arange(slots, dtype=jnp.int32)
    row_slot = jnp.zeros((rows,), jnp.int32).at[target].set(slot_ids)
    gate_buf = jnp.zeros((rows,), jnp.bfloat16).at[target].set(wt_all)
    dy_buf = cot_all[row_slot // top]
    hid_buf = hid_sl[row_slot]

    per_dest = n_grp * exp_dev * most
    dy_recv = lax.all_to_all(dy_buf.reshape(n_exp, per_dest, width), "exp", 0, 0, tiled=True)
    hid_recv = lax.all_to_all(hid_buf.reshape(n_exp, per_dest, f_loc), "exp", 0, 0, tiled=True)
    gate_recv = lax.all_to_all(gate_buf.reshape(n_exp, per_dest), "exp", 0, 0, tiled=True)
    dy_recv = dy_recv.reshape(n_exp, n_grp, exp_dev, most, width)
    hid_recv = hid_recv.reshape(n_exp, n_grp, exp_dev, most, f_loc)
    gate_f = gate_recv.reshape(n_exp, n_grp, exp_dev, most).astype(jnp.float32)

    proj = jnp.einsum("cgjmd,jfd->cgjmf", dy_recv, w_down, preferred_element_type=jnp.float32)
    dh_sl = (gate_f[..., None] * proj).astype(jnp.bfloat16)
    inner_p = jnp.sum(hid_recv.astype(jnp.float32) * proj, axis=4)
    scaled = (gate_f[..., None] * dy_recv.astype(jnp.float32)).astype(jnp.bfloat16)
    parts = jnp.einsum("cgjmf,cgjmd->gjfd", hid_recv, scaled, preferred_element_type=jnp.float32)
    d_weight = jnp.sum((parts * scale).astype(jnp.bfloat16).astype(jnp.float32), axis=0)

    dh_back = lax.all_to_all(dh_sl.reshape(n_exp, per_dest, f_loc), "exp", 0, 0, tiled=True)
    in_back = lax.all_to_all(inner_p.reshape(n_exp, per_dest), "exp", 0, 0, tiled=True)
    dh_slot = dh_back.reshape(rows, f_loc)[target].reshape(n_grp, tok, top, f_loc)
    in_slot = in_back.reshape(rows)[target].reshape(n_grp, tok, top)

    dh_home = lax.all_to_all(dh_slot, "grp", split_axis=0, concat_axis=0, tiled=True)
    d_hidden = jnp.transpose(dh_home, (1, 2, 0, 3)).reshape(tok, top, ffw)
    in_home = lax.all_to_all(in_slot, "grp", split_axis=0, concat_axis=0, tiled=True)
    inner = jnp.sum(in_home, axis=0).astype(jnp.bfloat16)
    d_gate = (inner.astype(jnp.float32) * live[:, None]).astype(jnp.bfloat16)
    return (d_hidden, d_gate, d_weight)


def solution(mesh):
    in_specs = (
        P(("grp", "exp"), None),
        P(("grp", "exp"), None, None),
        P(("grp", "exp"), None),
        P(("grp", "exp"), None),
        P("grp"),
        P("exp", "grp", None),
    )
    out_specs = (P(("grp", "exp"), None, None), P(("grp", "exp"), None), P("exp", "grp", None))
    return jax.shard_map(body, mesh=mesh, in_specs=in_specs, out_specs=out_specs, check_vma=False)
```

time: 502 us -> 379 us (0.75)
  waiting for transfers between devices: 388 us -> 105 us
  local copies, waits for them, and re-layouts: 34.2 us -> 98.7 us
  blocking collectives: 15.1 us -> 77.9 us
  starting transfers between devices: 23.7 us -> 37.9 us
  other arithmetic: 5.77 us -> 17.9 us
  matrix products: 16.6 us -> 24.2 us
    unnamed x3 -> x1, waiting for transfers between devices: 263 us -> 0.02 us
    all_gather x1, waiting for transfers between devices: 84 us -> 0.02 us  [body(): cot_all = lax.all_gather(cotangent, 'grp', tiled=True)]
    all_gather x0 -> x2, blocking collectives: none -> 72.3 us  [the longest x1 61.5 us: body(): ids_all = lax.all_gather(expert_ids, 'grp').reshape(n_grp, tok * top)]
    all_to_all x5 -> x8, waiting for transfers between devices: 41.6 us -> 105 us  [the longest x1 86.8 us: body(): lax.all_to_all(dy_buf.reshape(n_exp, per_dest, width), 'exp', 0, 0, tiled...]
    gather x2 -> x4, local copies, waits for them, and re-layouts: 5.64 us -> 48 us  [the longest x1 18 us: body(): dy_buf = cot_all[row_slot // top]]
    psum x1 -> x0, blocking collectives: 15.1 us -> none  [body(): total = lax.psum(count.astype(jnp.float32), 'grp')]
    all_to_all x5 -> x8, starting transfers between devices: 23.6 us -> 37.9 us  [the longest x1 6.31 us: body(): lax.all_to_all(dy_buf.reshape(n_exp, per_dest, width), 'exp', 0, 0, tiled...]
    reduce_sum x1 -> x4, other arithmetic: 0.09 us -> 11.9 us  [the longest x1 11.1 us: body(): jnp.sum((parts * scale).astype(jnp.bfloat16).astype(jnp.float32), axis=0)]
  transfers between devices with their start and end apart: 7 -> 9, of which waited for: 6 -> 5; matrix products, arithmetic and copies ran while one was open for 7% -> 33% of each run, Pallas kernels for 0% -> 0%
where the time goes in v2:
time: 379 us; the launch traced here: 378 us
  waiting for transfers between devices  105 us (28%)
  local copies, waits for them, and re-layouts  98.7 us (26%)
  blocking collectives  77.9 us (21%)
  starting transfers between devices  37.9 us (10%)
  matrix products  24.2 us (6%)
  other arithmetic  17.9 us (5%)
  between operations  15.6 us (4%)
    all_to_all x1, waiting for transfers between devices, body(): lax.all_to_all(dy_buf.reshape(n_exp, per_dest, width), 'exp', 0, 0, tiled...  86.8 us
    all_gather x1, blocking collectives, body(): ids_all = lax.all_gather(expert_ids, 'grp').reshape(n_grp, tok * top)  61.5 us
    gather x1, local copies, waits for them, and re-layouts, body(): dy_buf = cot_all[row_slot // top]  18 us
    dot_general x1, matrix products, body(): jnp.einsum('cgjmf,cgjmd->gjfd', hid_recv, scaled, preferred_element_type=...  14.8 us
    scatter x1, local copies, waits for them, and re-layouts, body(): gate_buf = jnp.zeros((rows,), jnp.bfloat16).at[target].set(wt_all)  14.6 us
    gather x1, local copies, waits for them, and re-layouts, body(): in_slot = in_back.reshape(rows)[target].reshape(n_grp, tok, top)  11.8 us
    reduce_sum x1, other arithmetic, body(): jnp.sum((parts * scale).astype(jnp.bfloat16).astype(jnp.float32), axis=0)  11.1 us
    all_gather x1, blocking collectives, body(): wt_all = lax.all_gather(weighted, 'grp').reshape(slots)  10.8 us
  transfers between devices with their start and end apart: 9, of which 5 were waited for; matrix products, arithmetic and copies ran while one was open for 33% of the time, Pallas kernels for 0%

profile of v2, /device:TPU:2, one launch (start us, length us, event | category | flops | bytes accessed | tf_op | source)
XLA Modules:
  0.0 377.6 jit_solution(17283104398827875300)
XLA Ops:
  7.2 0.0 copy-start
  7.2 2.7 copy.94
  9.9 5.0 %all-to-all-start.4 = ((bf16[4,128,4,360]{1,3,2,0:T(8,128)(2,1)}), bf16[4,128,4,360]{1,3,2,0:T(8,128)(2,1)}, u32[]{:S(2)}, u32[]{:S(2)}) async-start(bf16[4,128,4,360]{1,3,2,0:T(8,128)(2,1)} %copy.94), calls=%async_computation.4 | async-start | bytes 2949120 | tf_op jit(solution)/shard_map/all_to_all | solution.py:33
  14.9 0.9 copy.89
  15.9 0.0 all-gather.4.cloned.1.call-update
  15.9 61.5 %all-gather = s32[512,4]{0,1:T(4,128)S(1)} all-gather(s32[128,4]{0,1:T(4,128)S(1)} %copy-done.3), channel_id=2, replica_groups=mesh['grp'=4,'exp'=8] {'grp'}, dimensions={0}, use_global_device_ids=true | all-gather | bytes 10240 | tf_op jit(solution)/shard_map/all_gather | solution.py:30
  77.4 0.1 copy.82
  77.6 0.2 eq.31
  77.7 0.2 eq.27
  77.9 0.2 reshape.224
  78.8 0.0 copy-done.4
  78.8 10.8 %all-gather.1 = bf16[512,4]{0,1:T(4,128)(2,1)S(1)} all-gather(bf16[128,4]{0,1:T(4,128)(2,1)S(1)} %multiply_convert_fusion.2), channel_id=3, replica_groups=mesh['grp'=4,'exp'=8] {'grp'}, dimensions={0}, use_global_device_ids=true | all-gather | bytes 5120 | tf_op jit(solution)/shard_map/all_gather | solution.py:31
  89.6 0.2 copy.86
  89.8 0.2 reshape.276
  90.0 4.6 %reduce-window.6 = s32[4,16,4,128]{3,1,2,0:T(8,128)S(1)} reduce-window(s32[4,16,4,128]{3,1,2,0:T(8,128)S(1)} %fusion.12, s32[]{:T(128)} %constant.55.clone.1), window={size=1x1x1x128 pad=0_0x0_0x0_0x127_0}, to_apply=%region_0.0 | reduce-window | flops 4161536 | bytes 262148 | tf_op jit(solution)/shard_map/reduce-window
  94.6 0.4 slice_reduce_fusion
  95.1 0.1 fusion.11
  95.2 0.1 compare_select_fusion
  95.3 8.1 %scatter_custom_fusion.1 = s32[2560]{0:T(1024)S(1)} fusion(s32[2048]{0:T(1024)S(1)} %bitcast.73, s32[2048]{0:T(1024)S(1)} %iota.18, s32[]{:T(128)} %constant.55.clone.1), kind=kCustom, calls=%fused_computation.49 | custom fusion | bytes 10244 | tf_op jit(solution)/shard_map/scatter | solution.py:42
  103.4 14.6 %scatter_custom_fusion = bf16[2560]{0:T(1024)(128)(2,1)S(1)} fusion(s32[2048]{0:T(1024)S(1)} %bitcast.74, bf16[2048]{0:T(1024)(128)(2,1)S(1)} %reshape.276, bf16[]{:T(256)} %constant.53.clone.1), kind=kCustom, calls=%fused_computation.52 | custom fusion | bytes 5122 | tf_op jit(solution)/shard_map/scatter | solution.py:43
  118.0 0.1 all_to_all.40
  118.1 0.5 broadcast.189
  118.6 0.7 reduce.5
  119.3 0.7 reshape.310
  120.0 0.0 all-to-all-done.4
  120.0 4.3 %all-to-all-start = ((bf16[8,2,160]{2,1,0:T(2,128)(2,1)}), bf16[8,2,160]{2,1,0:T(2,128)(2,1)S(1)}, u32[]{:S(2)}, u32[]{:S(2)}) async-start(bf16[8,2,160]{2,1,0:T(2,128)(2,1)} %reshape.310), calls=%async_computation | async-start | bytes 16384 | tf_op jit(solution)/shard_map/all_to_all | solution.py:50
  124.3 3.7 copy.95
  127.9 3.7 reshape.234
  131.7 9.2 %gather_fusion.2 = bf16[2560,360]{1,0:T(8,128)(2,1)} fusion(bf16[2048,360]{1,0:T(8,128)(2,1)} %reshape.234, s32[3072]{0:T(1024)S(1)} %pad_clamp_fusion), kind=kCustom, calls=%fused_computation.2 | custom fusion | bytes 3696640 | tf_op jit(solution)/shard_map/gather | solution.py:45
  140.9 0.0 all-to-all-done
  140.9 4.3 %all-to-all-start.5 = ((bf16[8,320,360]{2,1,0:T(8,128)(2,1)}), bf16[8,320,360]{2,1,0:T(8,128)(2,1)}, u32[]{:S(2)}, u32[]{:S(2)}) async-start(bf16[8,320,360]{2,1,0:T(8,128)(2,1)} %bitcast.69), calls=%async_computation.5 | async-start | bytes 3932160 | tf_op jit(solution)/shard_map/all_to_all | solution.py:49
  145.2 0.0 all-gather.4.cloned.1.call-done
  145.2 18.0 %gather_fusion = bf16[2560,1440]{1,0:T(8,128)(2,1)} fusion(bf16[512,1440]{1,0:T(8,128)(2,1)} %all-gather.4.cloned.1.call-done, s32[3072]{0:T(1024)S(1)} %pad_clamp_fusion.1), kind=kCustom, calls=%fused_computation | custom fusion | bytes 14755840 | tf_op jit(solution)/shard_map/gather | solution.py:44
  163.2 5.8 %all-to-all-done.5 = bf16[8,320,360]{2,1,0:T(8,128)(2,1)} async-done(((bf16[8,320,360]{2,1,0:T(8,128)(2,1)}), bf16[8,320,360]{2,1,0:T(8,128)(2,1)}, u32[]{:S(2)}, u32[]{:S(2)}) %all-to-all-start.5) | async-done | bytes 1843232 | tf_op jit(solution)/shard_map/all_to_all | solution.py:49
  169.0 6.3 %all-to-all-start.1 = ((bf16[8,320,1440]{2,1,0:T(8,128)(2,1)}), bf16[8,320,1440]{2,1,0:T(8,128)(2,1)}, u32[]{:S(2)}, u32[]{:S(2)}) async-start(bf16[8,320,1440]{2,1,0:T(8,128)(2,1)} %bitcast.67), calls=%async_computation.1 | async-start | bytes 15728640 | tf_op jit(solution)/shard_map/all_to_all | solution.py:48
  175.3 0.1 reshape.311
  175.4 0.1 reshape.239
  175.5 86.8 %all-to-all-done.1 = bf16[8,320,1440]{2,1,0:T(8,128)(2,1)} async-done(((bf16[8,320,1440]{2,1,0:T(8,128)(2,1)}), bf16[8,320,1440]{2,1,0:T(8,128)(2,1)}, u32[]{:S(2)}, u32[]{:S(2)}) %all-to-all-start.1) | async-done | bytes 7372832 | tf_op jit(solution)/shard_map/all_to_all | solution.py:48
  262.3 9.4 %fusion.6 = (f32[8,4,2,40]{3,1,0,2:T(4,128)S(1)}, bf16[8,4,2,40,360]{4,3,1,0,2:T(8,128)(2,1)}) fusion(bf16[8,4,2,40,360]{4,3,2,1,0:T(8,128)(2,1)} %bitcast.15, f32[8,4,2,40]{3,1,0,2:T(4,128)S(1)} %copy.88, bf16[2,360,1440]{2,1,0:T(8,128)(2,1)S(1)} %copy-done, bf16[8,4,2,40,1440]{4,3,2,1,0:T(8,128)(2,1)} %bitcast.4), kind=kOutput, calls=%fused_computation.17 | convolution fusion | flops 2658813440 | bytes 13153280 | tf_op jit(solution)/shard_map/cgjmd,jfd->cgjmf/dot_general | solution.py:55
  271.8 0.7 all_to_all.41
  272.5 4.8 %all-to-all-start.6 = ((f32[8,1,320]{2,1,0:T(1,128)}), f32[8,1,320]{2,1,0:T(1,128)S(1)}, u32[]{:S(2)}, u32[]{:S(2)}) async-start(f32[8,1,320]{2,1,0:T(1,128)} %all_to_all.41), calls=%async_computation.6 | async-start | bytes 24576 | tf_op jit(solution)/shard_map/all_to_all | solution.py:63
  277.3 3.0 copy.91
  280.3 0.2 all-to-all-done.6
  280.6 5.0 %all-to-all-start.2 = ((bf16[8,320,360]{2,1,0:T(8,128)(2,1)}), bf16[8,320,360]{2,1,0:T(8,128)(2,1)S(1)}, u32[]{:S(2)}, u32[]{:S(2)}) async-start(bf16[8,320,360]{2,1,0:T(8,128)(2,1)} %bitcast.68), calls=%async_computation.2 | async-start | bytes 3932160 | tf_op jit(solution)/shard_map/all_to_all | solution.py:62
  285.6 0.6 dynamic-slice
  286.1 0.8 dynamic-update-slice
  286.9 5.6 %all-reduce = s32[4]{0:T(128)S(1)} all-reduce(s32[4]{0:T(128)S(1)} %dynamic-update-slice), channel_id=1, replica_groups=mesh['grp'=4,'exp'=8] {'grp'}, use_global_device_ids=true, to_apply=%add | all-reduce | flops 4 | bytes 32
  292.5 0.1 reshape.237
  292.6 11.8 %gather_fusion.3 = f32[2048]{0:T(1024)S(1)} fusion(f32[2560]{0:T(1024)S(1)} %reshape.237, s32[2048]{0:T(1024)S(1)} %broadcast_clamp_fusion), kind=kCustom, calls=%fused_computation.3 | custom fusion | bytes 24576 | tf_op jit(solution)/shard_map/gather | solution.py:65
  304.4 0.3 reshape.238
  304.6 0.7 copy.99
  305.3 3.9 %all-to-all-done.2 = bf16[8,320,360]{2,1,0:T(8,128)(2,1)S(1)} async-done(((bf16[8,320,360]{2,1,0:T(8,128)(2,1)}), bf16[8,320,360]{2,1,0:T(8,128)(2,1)S(1)}, u32[]{:S(2)}, u32[]{:S(2)}) %all-to-all-start.2) | async-done | bytes 1843232 | tf_op jit(solution)/shard_map/all_to_all | solution.py:62
  309.3 3.2 all-to-all-start.7
  312.5 0.6 convert_reduce_fusion.2
  313.8 9.1 %gather_fusion.1 = bf16[2048,360]{1,0:T(8,128)(2,1)} fusion(bf16[2560,360]{1,0:T(8,128)(2,1)S(1)} %bitcast.66, s32[2048]{0:T(1024)S(1)} %broadcast_clamp_fusion), kind=kCustom, calls=%fused_computation.1 | custom fusion | bytes 2957312 | tf_op jit(solution)/shard_map/gather | solution.py:64
  322.9 2.9 reshape.231
  325.8 2.4 copy.92
  328.2 0.0 all-to-all-done.7
  328.2 5.1 %all-to-all-start.3 = ((bf16[4,128,4,360]{1,3,2,0:T(8,128)(2,1)}), bf16[4,128,4,360]{1,3,2,0:T(8,128)(2,1)}, u32[]{:S(2)}, u32[]{:S(2)}) async-start(bf16[4,128,4,360]{1,3,2,0:T(8,128)(2,1)} %copy.92), calls=%async_computation.3 | async-start | bytes 2949120 | tf_op jit(solution)/shard_map/all_to_all | solution.py:67
  333.2 14.8 %fusion.1 = f32[4,2,360,1440,1]{3,2,0,1,4:T(8,128)} fusion(bf16[8,4,2,40,360]{4,3,2,1,0:T(8,128)(2,1)} %bitcast.15, bf16[8,4,2,40,1440]{4,3,2,1,0:T(8,128)(2,1)} %bitcast.4, f32[8,4,2,40]{3,2,1,0:T(2,128)S(1)} %reshape.239), kind=kOutput, calls=%fused_computation.10 | convolution fusion | flops 2665267200 | bytes 25815040 | tf_op jit(solution)/shard_map/cgjmf,cgjmd->gjfd/dot_general | solution.py:59
  348.0 11.1 %convert_reduce_fusion = f32[2,360,1440]{2,1,0:T(8,128)} fusion(f32[4,2,360,1440,1]{3,2,0,1,4:T(8,128)} %fusion.1, f32[]{:T(128)S(6)} %div.32), kind=kLoop, calls=%fused_computation.8 | loop fusion | flops 15552000 | bytes 20736004 | tf_op jit(solution)/shard_map/reduce_sum | solution.py:60
  359.2 0.6 multiply_convert_fusion.1
  359.7 8.4 %all-to-all-done.3 = bf16[4,128,4,360]{1,3,2,0:T(8,128)(2,1)} async-done(((bf16[4,128,4,360]{1,3,2,0:T(8,128)(2,1)}), bf16[4,128,4,360]{1,3,2,0:T(8,128)(2,1)}, u32[]{:S(2)}, u32[]{:S(2)}) %all-to-all-start.3) | async-done | bytes 1474592 | tf_op jit(solution)/shard_map/all_to_all | solution.py:67
  368.2 2.6 copy.93
  (30 shorter events, 0.3 us)
Async XLA Ops:
  7.2 255.2 %copy-start = (bf16[2,360,1440]{2,1,0:T(8,128)(2,1)S(1)}, bf16[2,360,1440]{2,1,0:T(8,128)(2,1)}, u32[]{:S(2)}) copy-start(bf16[2,360,1440]{2,1,0:T(8,128)(2,1)} %param.11) | copy-start | bytes 6220804
  7.2 7.8 %copy-start.2 = (bf16[128,1440]{0,1:T(8,128)(2,1)S(1)}, bf16[128,1440]{0,1:T(8,128)(2,1)}, u32[]{:S(2)}) copy-start(bf16[128,1440]{0,1:T(8,128)(2,1)} %param.6) | copy-start | bytes 1105924
  9.9 6.0 %copy-start.3 = (s32[128,4]{0,1:T(4,128)S(1)}, s32[128,4]{0,1:T(4,128)}, u32[]{:S(2)}) copy-start(s32[128,4]{0,1:T(4,128)} %param.9) | copy-start | bytes 6148
  9.9 68.9 %copy-start.4 = (bf16[128,4]{0,1:T(4,128)(2,1)S(1)}, bf16[128,4]{0,1:T(4,128)(2,1)}, u32[]{:S(2)}) copy-start(bf16[128,4]{0,1:T(4,128)(2,1)} %param.8) | copy-start | bytes 3076
  9.9 110.0 %all-to-all-start.4 = ((bf16[4,128,4,360]{1,3,2,0:T(8,128)(2,1)}), bf16[4,128,4,360]{1,3,2,0:T(8,128)(2,1)}, u32[]{:S(2)}, u32[]{:S(2)}) async-start(bf16[4,128,4,360]{1,3,2,0:T(8,128)(2,1)} %copy.94), calls=%async_computation.4 | async-start | bytes 2949120 | tf_op jit(solution)/shard_map/all_to_all | solution.py:33
  14.9 130.3 %all-gather.4.cloned.1.call-start = ((), (), s32[]{:S(2)}) async-start(), calls=%async_computation.8 | async-start | bytes 1966080 | tf_op jit(solution)/shard_map/all_gather | solution.py:29
  120.0 20.9 %all-to-all-start = ((bf16[8,2,160]{2,1,0:T(2,128)(2,1)}), bf16[8,2,160]{2,1,0:T(2,128)(2,1)S(1)}, u32[]{:S(2)}, u32[]{:S(2)}) async-start(bf16[8,2,160]{2,1,0:T(2,128)(2,1)} %reshape.310), calls=%async_computation | async-start | bytes 16384 | tf_op jit(solution)/shard_map/all_to_all | solution.py:50
  140.9 28.1 %all-to-all-start.5 = ((bf16[8,320,360]{2,1,0:T(8,128)(2,1)}), bf16[8,320,360]{2,1,0:T(8,128)(2,1)}, u32[]{:S(2)}, u32[]{:S(2)}) async-start(bf16[8,320,360]{2,1,0:T(8,128)(2,1)} %bitcast.69), calls=%async_computation.5 | async-start | bytes 3932160 | tf_op jit(solution)/shard_map/all_to_all | solution.py:49
  169.0 93.4 %all-to-all-start.1 = ((bf16[8,320,1440]{2,1,0:T(8,128)(2,1)}), bf16[8,320,1440]{2,1,0:T(8,128)(2,1)}, u32[]{:S(2)}, u32[]{:S(2)}) async-start(bf16[8,320,1440]{2,1,0:T(8,128)(2,1)} %bitcast.67), calls=%async_computation.1 | async-start | bytes 15728640 | tf_op jit(solution)/shard_map/all_to_all | solution.py:48
  272.5 8.1 %all-to-all-start.6 = ((f32[8,1,320]{2,1,0:T(1,128)}), f32[8,1,320]{2,1,0:T(1,128)S(1)}, u32[]{:S(2)}, u32[]{:S(2)}) async-start(f32[8,1,320]{2,1,0:T(1,128)} %all_to_all.41), calls=%async_computation.6 | async-start | bytes 24576 | tf_op jit(solution)/shard_map/all_to_all | solution.py:63
  280.3 5.2 %copy-start.5 = (u32[32]{0:T(128)S(1)}, u32[32]{0:T(128)}, u32[]{:S(2)}) copy-start(u32[32]{0:T(128)} %constant.72) | copy-start | bytes 388
  280.6 28.7 %all-to-all-start.2 = ((bf16[8,320,360]{2,1,0:T(8,128)(2,1)}), bf16[8,320,360]{2,1,0:T(8,128)(2,1)S(1)}, u32[]{:S(2)}, u32[]{:S(2)}) async-start(bf16[8,320,360]{2,1,0:T(8,128)(2,1)} %bitcast.68), calls=%async_computation.2 | async-start | bytes 3932160 | tf_op jit(solution)/shard_map/all_to_all | solution.py:62
  309.3 18.9 %all-to-all-start.7 = ((f32[4,128,4]{1,2,0:T(4,128)}), f32[4,128,4]{1,2,0:T(4,128)S(1)}, u32[]{:S(2)}, u32[]{:S(2)}) async-start(f32[4,128,4]{1,2,0:T(4,128)} %copy.99), calls=%async_computation.7 | async-start | bytes 16384 | tf_op jit(solution)/shard_map/all_to_all | solution.py:69
  328.2 40.0 %all-to-all-start.3 = ((bf16[4,128,4,360]{1,3,2,0:T(8,128)(2,1)}), bf16[4,128,4,360]{1,3,2,0:T(8,128)(2,1)}, u32[]{:S(2)}, u32[]{:S(2)}) async-start(bf16[4,128,4,360]{1,3,2,0:T(8,128)(2,1)} %copy.92), calls=%async_computation.3 | async-start | bytes 2949120 | tf_op jit(solution)/shard_map/all_to_all | solution.py:67
  348.0 22.7 %copy-start.1 = (bf16[2,360,1440]{2,1,0:T(8,128)(2,1)S(1)}, bf16[2,360,1440]{2,1,0:T(8,128)(2,1)}, u32[]{:S(2)}) copy-start(bf16[2,360,1440]{2,1,0:T(8,128)(2,1)} %param.11) | copy-start | bytes 6220804
Sparse Core Ops, SparseCore 0:
  17.3 58.1 all-gather.3

commit v3 on v1

--- a/solution.py
+++ b/solution.py
@@ -4,6 +4,21 @@
 from jax.sharding import PartitionSpec as P
 
 LOSS_SCALE = 32768
+
+
+def line_reduce_scatter(parts, n):
+    me = lax.axis_index("grp")
+    right = jnp.zeros(parts.shape[1:], parts.dtype)
+    left = jnp.zeros(parts.shape[1:], parts.dtype)
+    for k in range(1, n):
+        s_r = jnp.minimum(me + n - k, n - 1)
+        s_l = jnp.maximum(me - n + k, 0)
+        send_r = (parts[s_r].astype(jnp.float32) + right.astype(jnp.float32)).astype(parts.dtype)
+        send_l = (parts[s_l].astype(jnp.float32) + left.astype(jnp.float32)).astype(parts.dtype)
+        right = lax.ppermute(send_r, "grp", [(g, g + 1) for g in range(k)])
+        left = lax.ppermute(send_l, "grp", [(g, g - 1) for g in range(n - k, n)])
+    own = parts[me].astype(jnp.float32)
+    return own + right.astype(jnp.float32) + left.astype(jnp.float32)
 
 
 def body(cotangent, hidden, gates, expert_ids, group_counts, w_down):
@@ -59,12 +74,8 @@
         )
         * scale
     )
-    grad_rows = partial_grad.astype(jnp.bfloat16).reshape(ffw * exp_dev, width)
-    d_weight = (
-        lax.psum_scatter(grad_rows, "grp", scatter_dimension=0, tiled=True)
-        .reshape(exp_dev, ffw // n_grp, width)
-        .astype(jnp.float32)
-    )
+    grad_parts = partial_grad.astype(jnp.bfloat16).reshape(n_grp, exp_dev * (ffw // n_grp), width)
+    d_weight = line_reduce_scatter(grad_parts, n_grp).reshape(exp_dev, ffw // n_grp, width)
     back_dh, back_inner = (
         lax.all_to_all(
             dh_rows.reshape(n_exp, exp_dev * most, ffw),

time: 334 us -> 422 us (1.26)
  waiting for transfers between devices: 211 us -> 254 us
  starting transfers between devices: 23.7 us -> 44.9 us
  other arithmetic: 6.37 us -> 24.6 us
  local copies, waits for them, and re-layouts: 47.4 us -> 54.1 us
    ppermute x0 -> x6, waiting for transfers between devices: none -> 231 us  [the longest x3 176 us: line_reduce_scatter(): right = lax.ppermute(send_r, 'grp', [(g, g + 1) for g in range(k)])]
    reduce_scatter x1 -> x0, waiting for transfers between devices: 102 us -> none  [body(): lax.psum_scatter(grad_rows, 'grp', scatter_dimension=0, tiled=True)]
    all_gather x1, waiting for transfers between devices: 65.4 us -> 0.02 us  [body(): lax.all_gather(w_down, 'grp', axis=1, tiled=True)]
    ppermute x0 -> x6, starting transfers between devices: none -> 21.4 us  [the longest x3 15.8 us: line_reduce_scatter(): right = lax.ppermute(send_r, 'grp', [(g, g + 1) for g in range(k)])]
    all_to_all x1, waiting for transfers between devices: 19.3 us -> 0.01 us  [body(): lax.all_to_all(dh_rows.reshape(n_exp, exp_dev * most, ffw), 'exp', split_...]
    convert_element_type x1 -> x3, other arithmetic: 4.31 us -> 15.4 us  [the longest x2 11.1 us: line_reduce_scatter(): (parts[s_r].astype(jnp.float32) + right.astype(jnp.float32)).astype(parts...]
    add x0 -> x1, other arithmetic: none -> 5.82 us  [line_reduce_scatter(): return own + right.astype(jnp.float32) + left.astype(jnp.float32)]
    squeeze x0 -> x1, local copies, waits for them, and re-layouts: none -> 4.73 us  [line_reduce_scatter(): parts[s_r].astype(jnp.float32) + right.astype(jnp.float32)]
  transfers between devices with their start and end apart: 7 -> 12, of which waited for: 6 -> 7; matrix products, arithmetic and copies ran while one was open for 21% -> 20% of each run, Pallas kernels for 0% -> 0%
where the time goes in v3:
time: 422 us
  waiting for transfers between devices  254 us (60%)
  local copies, waits for them, and re-layouts  54.1 us (13%)
  starting transfers between devices  44.9 us (11%)
  other arithmetic  24.6 us (6%)
  matrix products  19.3 us (5%)
  between operations  15.5 us (4%)
  blocking collectives  8.61 us (2%)
    ppermute x3, waiting for transfers between devices, line_reduce_scatter(): right = lax.ppermute(send_r, 'grp', [(g, g + 1) for g in range(k)])  176 us
    ppermute x3, waiting for transfers between devices, line_reduce_scatter(): left = lax.ppermute(send_l, 'grp', [(g, g - 1) for g in range(n - k, n)])  54.5 us
    ppermute x3, starting transfers between devices, line_reduce_scatter(): right = lax.ppermute(send_r, 'grp', [(g, g + 1) for g in range(k)])  15.8 us
    all_to_all x1, waiting for transfers between devices, body(): lax.all_to_all(hid_buf, 'exp', split_axis=0, concat_axis=0, tiled=True)  13.3 us
    convert_element_type x2, other arithmetic, line_reduce_scatter(): (parts[s_r].astype(jnp.float32) + right.astype(jnp.float32)).astype(parts...  11.1 us
    dot_general x1, matrix products, body(): jnp.einsum('sjmgf,sjmd->gjfd', hid_four.reshape(n_exp, exp_dev, most, n_g...  10.5 us
    scatter x1, local copies, waits for them, and re-layouts, body(): jnp.zeros((experts * most, width), jnp.bfloat16).at[target]  9.55 us
    all_to_all x1, waiting for transfers between devices, body(): lax.all_to_all(dy_buf, 'exp', split_axis=0, concat_axis=0, tiled=True)  9.5 us
  transfers between devices with their start and end apart: 12, of which 7 were waited for; matrix products, arithmetic and copies ran while one was open for 20% of the time, Pallas kernels for 0%

profile of v3, /device:TPU:2, one launch (start us, length us, event | category | flops | bytes accessed | tf_op | source)
XLA Modules:
  0.0 421.5 jit_solution(4963763519141922327)
XLA Ops:
  7.2 0.7 broadcast_multiply_fusion
  7.8 0.8 copy.47
  8.6 0.1 eq.25
  8.7 0.1 eq.29
  8.9 0.1 copy.46
  9.0 0.1 mul.62
  9.1 1.2 reduce-window.6
  10.2 0.2 slice_reduce_fusion
  11.2 0.7 convert_multiply_fusion
  11.9 0.1 copy.51
  12.0 0.1 reshape.227
  12.1 0.1 fusion.24
  12.2 3.8 scatter_custom_fusion
  16.0 0.7 all_to_all.25
  16.7 4.3 %all-to-all-start = ((bf16[8,1,80]{2,1,0:T(2,128)(2,1)}), bf16[8,1,80]{2,1,0:T(2,128)(2,1)S(1)}, u32[]{:S(2)}, u32[]{:S(2)}) async-start(bf16[8,1,80]{2,1,0:T(2,128)(2,1)} %all_to_all.25), calls=%async_computation | async-start | bytes 8192 | tf_op jit(solution)/shard_map/all_to_all | solution.py:53
  20.9 2.9 copy.57
  23.8 0.8 reshape.243
  24.6 4.5 %scatter_custom_fusion.2 = bf16[640,1440]{1,0:T(8,128)(2,1)} fusion(s32[512]{0:T(512)S(1)} %bitcast.93, bf16[512,1440]{1,0:T(8,128)(2,1)S(1)} %reshape.243, bf16[]{:T(256)} %constant.51.clone.1), kind=kCustom, calls=%fused_computation.35 | custom fusion | bytes 1843202 | tf_op jit(solution)/shard_map/scatter | solution.py:46
  29.1 4.3 %all-to-all-start.3 = ((bf16[8,80,1440]{2,1,0:T(8,128)(2,1)}), bf16[8,80,1440]{2,1,0:T(8,128)(2,1)S(1)}, u32[]{:S(2)}, u32[]{:S(2)}) async-start(bf16[8,80,1440]{2,1,0:T(8,128)(2,1)} %bitcast.90), calls=%async_computation.3 | async-start | bytes 3932160 | tf_op jit(solution)/shard_map/all_to_all | solution.py:55
  33.5 0.0 all-gather.2.cloned.1.call-start
  33.5 0.7 all-gather.2.cloned.1.call-update
  34.2 0.2 copy.54
  34.4 9.6 %scatter_custom_fusion.1 = bf16[640,1440]{1,0:T(8,128)(2,1)} fusion(s32[512]{0:T(512)S(1)} %bitcast.94, bf16[128,1440]{1,0:T(8,128)(2,1)S(1)} %copy.54, s32[1024]{0:T(1024)S(1)} %pad_clamp_fusion.1, bf16[]{:T(256)} %constant.51.clone.1), kind=kCustom, calls=%fused_computation.33 | custom fusion | bytes 1843202 | tf_op jit(solution)/shard_map/scatter | solution.py:45
  44.0 13.3 %all-to-all-done.3 = bf16[8,80,1440]{2,1,0:T(8,128)(2,1)S(1)} async-done(((bf16[8,80,1440]{2,1,0:T(8,128)(2,1)}), bf16[8,80,1440]{2,1,0:T(8,128)(2,1)S(1)}, u32[]{:S(2)}, u32[]{:S(2)}) %all-to-all-start.3) | async-done | bytes 1843232 | tf_op jit(solution)/shard_map/all_to_all | solution.py:55
  57.2 5.7 %all-to-all-start.1 = ((bf16[8,80,1440]{2,1,0:T(8,128)(2,1)}), bf16[8,80,1440]{2,1,0:T(8,128)(2,1)}, u32[]{:S(2)}, u32[]{:S(2)}) async-start(bf16[8,80,1440]{2,1,0:T(8,128)(2,1)} %bitcast.88), calls=%async_computation.1 | async-start | bytes 3932160 | tf_op jit(solution)/shard_map/all_to_all | solution.py:52
  62.9 0.6 dynamic-slice
  63.5 0.8 dynamic-update-slice
  64.3 8.6 %all-reduce = s32[4]{0:T(128)S(1)} all-reduce(s32[4]{0:T(128)S(1)} %dynamic-update-slice), channel_id=1, replica_groups=mesh['grp'=4,'exp'=8] {'grp'}, use_global_device_ids=true, to_apply=%add | all-reduce | flops 4 | bytes 32
  72.9 0.6 convert_reduce_fusion.1
  74.2 0.1 reshape.191
  74.3 3.0 reshape_reshape.3
  77.3 9.5 %all-to-all-done.1 = bf16[8,80,1440]{2,1,0:T(8,128)(2,1)} async-done(((bf16[8,80,1440]{2,1,0:T(8,128)(2,1)}), bf16[8,80,1440]{2,1,0:T(8,128)(2,1)}, u32[]{:S(2)}, u32[]{:S(2)}) %all-to-all-start.1) | async-done | bytes 1843232 | tf_op jit(solution)/shard_map/all_to_all | solution.py:52
  86.8 10.5 %fusion.1 = bf16[4,2,360,1440]{3,2,0,1:T(8,128)(2,1)} fusion(f32[]{:T(128)S(6)} %div.13, bf16[8,2,40,4,360]{4,3,2,1,0:T(4,128)(2,1)} %reshape_reshape.3, f32[8,2,40]{2,0,1:T(8,128)S(1)} %copy.53, bf16[8,2,40,1440]{3,2,1,0:T(8,128)(2,1)} %bitcast.6), kind=kOutput, calls=%fused_computation.8 | convolution fusion | flops 2665267200 | bytes 11983364 | tf_op jit(solution)/shard_map/sjmgf,sjmd->gjfd/dot_general | solution.py:69
  97.3 7.8 %copy.63 = bf16[4,2,360,1440]{3,2,1,0:T(8,128)(2,1)} copy(bf16[4,2,360,1440]{3,2,0,1:T(8,128)(2,1)} %fusion.1) | data formatting | bytes 16588800 | tf_op jit(solution)/shard_map/convert_element_type | solution.py:77
  105.2 4.7 %dynamic-slice_bitcast_fusion.1 = (bf16[720,1440]{1,0:T(8,128)(2,1)}, bf16[720,1440]{1,0:T(8,128)(2,1)}) fusion(bf16[4,720,1440]{2,1,0:T(8,128)(2,1)} %bitcast.82, s32[]{:T(128)S(6)} %select_n.57, s32[]{:T(128)S(6)} %max.11), kind=kLoop, calls=%fused_computation.27 | loop fusion | bytes 8294408 | tf_op jit(solution)/shard_map/squeeze | solution.py:16
  109.9 5.0 %collective-permute-start = (bf16[720,1440]{1,0:T(8,128)(2,1)}, bf16[720,1440]{1,0:T(8,128)(2,1)}, u32[]{:S(2)}, u32[]{:S(2)}) collective-permute-start(bf16[720,1440]{1,0:T(8,128)(2,1)} %get-tuple-element.17), channel_id=1, source_target_pairs={{0,8},{1,9},{2,10},{3,11},{4,12},{5,13},{6,14},{7,15}} | collective-permute-start | bytes 6220808 | tf_op jit(solution)/shard_map/ppermute | solution.py:18
  114.8 2.0 collective-permute-start.3
  116.9 92.4 %collective-permute-done = bf16[720,1440]{1,0:T(8,128)(2,1)} collective-permute-done((bf16[720,1440]{1,0:T(8,128)(2,1)}, bf16[720,1440]{1,0:T(8,128)(2,1)}, u32[]{:S(2)}, u32[]{:S(2)}) %collective-permute-start) | collective-permute-done | bytes 2073632 | tf_op jit(solution)/shard_map/ppermute | solution.py:18
  209.3 4.2 fusion.6
  213.5 5.8 %collective-permute-start.1 = (bf16[720,1440]{1,0:T(8,128)(2,1)}, bf16[720,1440]{1,0:T(8,128)(2,1)}, u32[]{:S(2)}, u32[]{:S(2)}) collective-permute-start(bf16[720,1440]{1,0:T(8,128)(2,1)} %fusion.6), channel_id=1, source_target_pairs={{0,8},{8,16},{1,9},{9,17},{2,10},{10,18},{3,11},{11,19},{4,12},{12... | collective-permute-start | bytes 6220808 | tf_op jit(solution)/shard_map/ppermute | solution.py:18
  219.3 65.6 %collective-permute-done.1 = bf16[720,1440]{1,0:T(8,128)(2,1)} collective-permute-done((bf16[720,1440]{1,0:T(8,128)(2,1)}, bf16[720,1440]{1,0:T(8,128)(2,1)}, u32[]{:S(2)}, u32[]{:S(2)}) %collective-permute-start.1) | collective-permute-done | bytes 2073632 | tf_op jit(solution)/shard_map/ppermute | solution.py:18
  284.9 6.9 %fusion.7 = (bf16[720,1440]{1,0:T(8,128)(2,1)}, bf16[720,1440]{1,0:T(8,128)(2,1)}) fusion(bf16[720,1440]{1,0:T(8,128)(2,1)} %collective-permute-done.1, bf16[4,720,1440]{2,1,0:T(8,128)(2,1)} %bitcast.84, s32[]{:T(128)S(6)} %select_n.55, bf16[720,1440]{1,0:T(8,128)(2,1)} %collective-permute-done.3, s32[]{:T(128)S(6)} %max.10), kind=kLoop, calls=%fused_computation.18 | loop fusion | flops 8294400 | bytes 12441608 | tf_op jit(solution)/shard_map/convert_element_type | solution.py:16
  291.9 2.0 collective-permute-start.4
  293.9 5.0 %collective-permute-start.2 = (bf16[720,1440]{1,0:T(8,128)(2,1)}, bf16[720,1440]{1,0:T(8,128)(2,1)}, u32[]{:S(2)}, u32[]{:S(2)}) collective-permute-start(bf16[720,1440]{1,0:T(8,128)(2,1)} %get-tuple-element.15), channel_id=1, source_target_pairs={{0,8},{8,16},{16,24},{1,9},{9,17},{17,25},{2,10},{10,18},{18,26},{... | collective-permute-start | bytes 6220808 | tf_op jit(solution)/shard_map/ppermute | solution.py:18
  298.9 4.3 %fusion.5 = bf16[720,1440]{1,0:T(8,128)(2,1)} fusion(bf16[720,1440]{1,0:T(8,128)(2,1)} %collective-permute-done.4, bf16[4,720,1440]{2,1,0:T(8,128)(2,1)} %bitcast.85, s32[]{:T(128)S(6)} %max.9), kind=kLoop, calls=%fused_computation.14 | loop fusion | flops 4147200 | bytes 6220804 | tf_op jit(solution)/shard_map/convert_element_type | solution.py:17
  303.2 1.5 collective-permute-start.5
  304.8 0.0 all-gather.2.cloned.1.call-done
  304.8 8.8 %fusion.10 = (bf16[8,2,40]{2,0,1:T(8,128)(2,1)S(1)}, bf16[8,2,40,1440]{3,2,0,1:T(8,128)(2,1)}) fusion(f32[8,2,40]{2,0,1:T(8,128)S(1)} %copy.53, bf16[2,1440,1440]{2,1,0:T(8,128)(2,1)} %all-gather.2.cloned.1.call-done, bf16[8,2,40,1440]{3,2,1,0:T(8,128)(2,1)} %bitcast.6, bf16[8,2,40,1440]{3,2,1,0:T(8,128)(2,1)S(1)} %bitcast.87), kind=kOutput, calls=%fused_computation.24 | convolution fusion | flops 2658815488 | bytes 13827840 | tf_op jit(solution)/shard_map/sjmd,jfd->sjmf/dot_general | solution.py:59
  313.6 0.7 convert_element_type.192
  314.3 4.2 all-to-all-start.4
  318.5 3.0 copy.56
  321.5 0.1 all-to-all-done.4
  321.6 5.0 %all-to-all-start.2 = ((bf16[8,80,1440]{2,1,0:T(8,128)(2,1)}), bf16[8,80,1440]{2,1,0:T(8,128)(2,1)S(1)}, u32[]{:S(2)}, u32[]{:S(2)}) async-start(bf16[8,80,1440]{2,1,0:T(8,128)(2,1)} %bitcast.89), calls=%async_computation.2 | async-start | bytes 3932160 | tf_op jit(solution)/shard_map/all_to_all | solution.py:80
  326.6 18.3 %collective-permute-done.2 = bf16[720,1440]{1,0:T(8,128)(2,1)} collective-permute-done((bf16[720,1440]{1,0:T(8,128)(2,1)}, bf16[720,1440]{1,0:T(8,128)(2,1)}, u32[]{:S(2)}, u32[]{:S(2)}) %collective-permute-start.2) | collective-permute-done | bytes 2073632 | tf_op jit(solution)/shard_map/ppermute | solution.py:18
  344.9 54.5 %collective-permute-done.5 = bf16[720,1440]{1,0:T(8,128)(2,1)} collective-permute-done((bf16[720,1440]{1,0:T(8,128)(2,1)}, bf16[720,1440]{1,0:T(8,128)(2,1)}, u32[]{:S(2)}, u32[]{:S(2)}) %collective-permute-start.5) | collective-permute-done | bytes 2073632 | tf_op jit(solution)/shard_map/ppermute | solution.py:19
  399.4 5.8 %fusion.8 = f32[720,1440]{1,0:T(8,128)} fusion(bf16[720,1440]{1,0:T(8,128)(2,1)} %collective-permute-done.5, bf16[720,1440]{1,0:T(8,128)(2,1)} %collective-permute-done.2, bf16[4,720,1440]{2,1,0:T(8,128)(2,1)} %bitcast.86, s32[]{:T(128)S(6)} %select_n.54), kind=kLoop, calls=%fused_computation.20 | loop fusion | flops 5184000 | bytes 10368004 | tf_op jit(solution)/shard_map/add | solution.py:21
  405.2 0.1 reshape.188
  405.3 3.5 gather_fusion.1
  408.8 0.1 reshape.193
  408.9 0.1 multiply_convert_fusion.1
  409.0 0.7 copy.65
  409.7 2.1 gather_fusion
  411.8 0.4 reshape.185
  412.3 2.4 copy.64
  (20 shorter events, 0.1 us)
Async XLA Ops:
  16.7 12.4 %all-to-all-start = ((bf16[8,1,80]{2,1,0:T(2,128)(2,1)}), bf16[8,1,80]{2,1,0:T(2,128)(2,1)S(1)}, u32[]{:S(2)}, u32[]{:S(2)}) async-start(bf16[8,1,80]{2,1,0:T(2,128)(2,1)} %all_to_all.25), calls=%async_computation | async-start | bytes 8192 | tf_op jit(solution)/shard_map/all_to_all | solution.py:53
  29.1 5.1 %copy-start = (bf16[128,1440]{0,1:T(8,128)(2,1)S(1)}, bf16[128,1440]{0,1:T(8,128)(2,1)}, u32[]{:S(2)}) copy-start(bf16[128,1440]{0,1:T(8,128)(2,1)} %param.6) | copy-start | bytes 1105924
  29.1 28.1 %all-to-all-start.3 = ((bf16[8,80,1440]{2,1,0:T(8,128)(2,1)}), bf16[8,80,1440]{2,1,0:T(8,128)(2,1)S(1)}, u32[]{:S(2)}, u32[]{:S(2)}) async-start(bf16[8,80,1440]{2,1,0:T(8,128)(2,1)} %bitcast.90), calls=%async_computation.3 | async-start | bytes 3932160 | tf_op jit(solution)/shard_map/all_to_all | solution.py:55
  33.5 271.3 %all-gather.2.cloned.1.call-start = ((), (), s32[]{:S(2)}) async-start(), calls=%async_computation.5 | async-start | bytes 11059200 | tf_op jit(solution)/shard_map/all_gather | solution.py:62
  43.9 19.0 %copy-start.1 = (u32[32]{0:T(128)S(1)}, u32[32]{0:T(128)}, u32[]{:S(2)}) copy-start(u32[32]{0:T(128)} %constant.71) | copy-start | bytes 388
  57.2 29.6 %all-to-all-start.1 = ((bf16[8,80,1440]{2,1,0:T(8,128)(2,1)}), bf16[8,80,1440]{2,1,0:T(8,128)(2,1)}, u32[]{:S(2)}, u32[]{:S(2)}) async-start(bf16[8,80,1440]{2,1,0:T(8,128)(2,1)} %bitcast.88), calls=%async_computation.1 | async-start | bytes 3932160 | tf_op jit(solution)/shard_map/all_to_all | solution.py:52
  109.9 99.4 %collective-permute-start = (bf16[720,1440]{1,0:T(8,128)(2,1)}, bf16[720,1440]{1,0:T(8,128)(2,1)}, u32[]{:S(2)}, u32[]{:S(2)}) collective-permute-start(bf16[720,1440]{1,0:T(8,128)(2,1)} %get-tuple-element.17), channel_id=1, source_target_pairs={{0,8},{1,9},{2,10},{3,11},{4,12},{5,13},{6,14},{7,15}} | collective-permute-start | bytes 6220808 | tf_op jit(solution)/shard_map/ppermute | solution.py:18
  114.8 104.5 %collective-permute-start.3 = (bf16[720,1440]{1,0:T(8,128)(2,1)}, bf16[720,1440]{1,0:T(8,128)(2,1)}, u32[]{:S(2)}, u32[]{:S(2)}) collective-permute-start(bf16[720,1440]{1,0:T(8,128)(2,1)} %get-tuple-element.18), channel_id=1, source_target_pairs={{24,16},{25,17},{26,18},{27,19},{28,20},{29,21},{30,22},{31,23}} | collective-permute-start | bytes 6220808 | tf_op jit(solution)/shard_map/ppermute | solution.py:19
  213.5 71.4 %collective-permute-start.1 = (bf16[720,1440]{1,0:T(8,128)(2,1)}, bf16[720,1440]{1,0:T(8,128)(2,1)}, u32[]{:S(2)}, u32[]{:S(2)}) collective-permute-start(bf16[720,1440]{1,0:T(8,128)(2,1)} %fusion.6), channel_id=1, source_target_pairs={{0,8},{8,16},{1,9},{9,17},{2,10},{10,18},{3,11},{11,19},{4,12},{12... | collective-permute-start | bytes 6220808 | tf_op jit(solution)/shard_map/ppermute | solution.py:18
  291.9 7.1 %collective-permute-start.4 = (bf16[720,1440]{1,0:T(8,128)(2,1)}, bf16[720,1440]{1,0:T(8,128)(2,1)}, u32[]{:S(2)}, u32[]{:S(2)}) collective-permute-start(bf16[720,1440]{1,0:T(8,128)(2,1)} %get-tuple-element.16), channel_id=1, source_target_pairs={{16,8},{24,16},{17,9},{25,17},{18,10},{26,18},{19,11},{27,19},{20,... | collective-permute-start | bytes 6220808 | tf_op jit(solution)/shard_map/ppermute | solution.py:19
  293.9 51.0 %collective-permute-start.2 = (bf16[720,1440]{1,0:T(8,128)(2,1)}, bf16[720,1440]{1,0:T(8,128)(2,1)}, u32[]{:S(2)}, u32[]{:S(2)}) collective-permute-start(bf16[720,1440]{1,0:T(8,128)(2,1)} %get-tuple-element.15), channel_id=1, source_target_pairs={{0,8},{8,16},{16,24},{1,9},{9,17},{17,25},{2,10},{10,18},{18,26},{... | collective-permute-start | bytes 6220808 | tf_op jit(solution)/shard_map/ppermute | solution.py:18
  303.2 96.2 %collective-permute-start.5 = (bf16[720,1440]{1,0:T(8,128)(2,1)}, bf16[720,1440]{1,0:T(8,128)(2,1)}, u32[]{:S(2)}, u32[]{:S(2)}) collective-permute-start(bf16[720,1440]{1,0:T(8,128)(2,1)} %fusion.5), channel_id=1, source_target_pairs={{8,0},{16,8},{24,16},{9,1},{17,9},{25,17},{10,2},{18,10},{26,18},{... | collective-permute-start | bytes 6220808 | tf_op jit(solution)/shard_map/ppermute | solution.py:19
  314.3 7.3 %all-to-all-start.4 = ((bf16[8,1,80]{2,1,0:T(2,128)(2,1)}), bf16[8,1,80]{2,1,0:T(2,128)(2,1)S(1)}, u32[]{:S(2)}, u32[]{:S(2)}) async-start(bf16[8,1,80]{2,1,0:T(2,128)(2,1)} %convert_element_type.192), calls=%async_computation.4 | async-start | bytes 8192 | tf_op jit(solution)/shard_map/all_to_all | solution.py:87
  321.6 88.1 %all-to-all-start.2 = ((bf16[8,80,1440]{2,1,0:T(8,128)(2,1)}), bf16[8,80,1440]{2,1,0:T(8,128)(2,1)S(1)}, u32[]{:S(2)}, u32[]{:S(2)}) async-start(bf16[8,80,1440]{2,1,0:T(8,128)(2,1)} %bitcast.89), calls=%async_computation.2 | async-start | bytes 3932160 | tf_op jit(solution)/shard_map/all_to_all | solution.py:80
Sparse Core Ops, SparseCore 0:
  35.9 221.3 all-gather.1

commit v4 on v3

--- a/solution.py
+++ b/solution.py
@@ -4,6 +4,19 @@
 from jax.sharding import PartitionSpec as P
 
 LOSS_SCALE = 32768
+
+
+def line_all_gather(shard, n):
+    me = lax.axis_index("grp")
+    from_left, from_right = [], []
+    go_r = go_l = shard
+    for k in range(1, n):
+        go_r = lax.ppermute(go_r, "grp", [(g, g + 1) for g in range(k - 1, n - 1)])
+        go_l = lax.ppermute(go_l, "grp", [(g, g - 1) for g in range(1, n - k + 1)])
+        from_left.append(go_r)
+        from_right.append(go_l)
+    pieces = jnp.stack(from_left[::-1] + [shard] + from_right)
+    return lax.dynamic_slice_in_dim(pieces, n - 1 - me, n, axis=0)
 
 
 def line_reduce_scatter(parts, n):
@@ -59,7 +72,7 @@
     proj = jnp.einsum(
         "sjmd,jfd->sjmf",
         dy_four,
-        lax.all_gather(w_down, "grp", axis=1, tiled=True),
+        jnp.transpose(line_all_gather(w_down, n_grp), (1, 0, 2, 3)).reshape(exp_dev, ffw, width),
         preferred_element_type=jnp.float32,
     )
     dh_rows = (gate_three[..., None] * proj).astype(jnp.bfloat16)

time: 422 us -> 375 us (0.89)
  the two profiles are of different devices: /device:TPU:2 before, /device:TPU:24 now
where the time goes in v4:
time: 375 us; the launch traced here: 368 us
  starting transfers between devices  106 us (28%)
  local copies, waits for them, and re-layouts  88.1 us (23%)
  waiting for transfers between devices  80.8 us (22%)
  blocking collectives  46.7 us (12%)
  other arithmetic  24.6 us (7%)
  matrix products  19.1 us (5%)
    ppermute x3, starting transfers between devices, line_reduce_scatter(): left = lax.ppermute(send_l, 'grp', [(g, g - 1) for g in range(n - k, n)])  68 us
    unnamed x1, blocking collectives  46.7 us
    ppermute x3, waiting for transfers between devices, line_all_gather(): go_r = lax.ppermute(go_r, 'grp', [(g, g + 1) for g in range(k - 1, n - 1)])  35.3 us
    unnamed x20, local copies, waits for them, and re-layouts  25.8 us
    all_to_all x1, waiting for transfers between devices, body(): lax.all_to_all(dh_rows.reshape(n_exp, exp_dev * most, ffw), 'exp', split_...  20.7 us
    all_to_all x1, waiting for transfers between devices, body(): lax.all_to_all(hid_buf, 'exp', split_axis=0, concat_axis=0, tiled=True)  15.4 us
    transpose x2, local copies, waits for them, and re-layouts, body(): jnp.transpose(line_all_gather(w_down, n_grp), (1, 0, 2, 3))  15.2 us
    convert_element_type x2, other arithmetic, line_reduce_scatter(): (parts[s_r].astype(jnp.float32) + right.astype(jnp.float32)).astype(parts...  11.1 us
  transfers between devices with their start and end apart: 17, of which 5 were waited for; matrix products, arithmetic and copies ran while one was open for 32% of the time, Pallas kernels for 0%

profile of v4, /device:TPU:24, one launch (start us, length us, event | category | flops | bytes accessed | tf_op | source)
XLA Modules:
  0.0 368.0 jit_solution(11502779434400416642)
XLA Ops:
  0.6 0.7 broadcast_multiply_fusion
  1.3 0.8 copy.50
  2.6 1.2 reduce-window.6
  3.7 0.2 slice_reduce_fusion
  4.6 0.7 convert_multiply_fusion
  5.3 0.1 copy.54
  5.7 3.8 %scatter_custom_fusion = bf16[640]{0:T(1024)(128)(2,1)S(1)} fusion(s32[512]{0:T(512)S(1)} %bitcast.108, bf16[512]{0:T(512)(128)(2,1)S(1)} %reshape.231, bf16[]{:T(256)} %constant.53.clone.1), kind=kCustom, calls=%fused_computation.67 | custom fusion | bytes 1282 | tf_op jit(solution)/shard_map/scatter | solution.py:60
  9.5 0.7 all_to_all.25
  10.2 3.7 %all-to-all-start = ((bf16[8,1,80]{2,1,0:T(2,128)(2,1)}), bf16[8,1,80]{2,1,0:T(2,128)(2,1)S(1)}, u32[]{:S(2)}, u32[]{:S(2)}) async-start(bf16[8,1,80]{2,1,0:T(2,128)(2,1)} %all_to_all.25), calls=%async_computation | async-start | bytes 8192 | tf_op jit(solution)/shard_map/all_to_all | solution.py:66
  13.9 2.9 copy.61
  16.8 0.8 reshape.247
  17.5 4.5 %scatter_custom_fusion.2 = bf16[640,1440]{1,0:T(8,128)(2,1)} fusion(s32[512]{0:T(512)S(1)} %bitcast.109, bf16[512,1440]{1,0:T(8,128)(2,1)S(1)} %reshape.247, bf16[]{:T(256)} %constant.53.clone.1), kind=kCustom, calls=%fused_computation.42 | custom fusion | bytes 1843202 | tf_op jit(solution)/shard_map/scatter | solution.py:59
  22.0 4.5 %all-to-all-start.3 = ((bf16[8,80,1440]{2,1,0:T(8,128)(2,1)}), bf16[8,80,1440]{2,1,0:T(8,128)(2,1)S(1)}, u32[]{:S(2)}, u32[]{:S(2)}) async-start(bf16[8,80,1440]{2,1,0:T(8,128)(2,1)} %bitcast.106), calls=%async_computation.3 | async-start | bytes 3932160 | tf_op jit(solution)/shard_map/all_to_all | solution.py:68
  26.6 0.2 copy.58
  26.8 9.6 %scatter_custom_fusion.1 = bf16[640,1440]{1,0:T(8,128)(2,1)} fusion(s32[512]{0:T(512)S(1)} %bitcast.110, bf16[128,1440]{1,0:T(8,128)(2,1)S(1)} %copy.58, s32[1024]{0:T(1024)S(1)} %pad_clamp_fusion.1, bf16[]{:T(256)} %constant.53.clone.1), kind=kCustom, calls=%fused_computation.40 | custom fusion | bytes 1843202 | tf_op jit(solution)/shard_map/scatter | solution.py:58
  36.3 15.4 %all-to-all-done.3 = bf16[8,80,1440]{2,1,0:T(8,128)(2,1)S(1)} async-done(((bf16[8,80,1440]{2,1,0:T(8,128)(2,1)}), bf16[8,80,1440]{2,1,0:T(8,128)(2,1)S(1)}, u32[]{:S(2)}, u32[]{:S(2)}) %all-to-all-start.3) | async-done | bytes 1843232 | tf_op jit(solution)/shard_map/all_to_all | solution.py:68
  51.8 4.3 %all-to-all-start.1 = ((bf16[8,80,1440]{2,1,0:T(8,128)(2,1)}), bf16[8,80,1440]{2,1,0:T(8,128)(2,1)}, u32[]{:S(2)}, u32[]{:S(2)}) async-start(bf16[8,80,1440]{2,1,0:T(8,128)(2,1)} %bitcast.104), calls=%async_computation.1 | async-start | bytes 3932160 | tf_op jit(solution)/shard_map/all_to_all | solution.py:65
  56.1 1.3 collective-permute-start
  57.4 0.6 dynamic-slice
  58.0 0.8 dynamic-update-slice
  58.8 6.0 %collective-permute-start.3 = (bf16[2,360,1440]{2,1,0:T(8,128)(2,1)}, bf16[2,360,1440]{2,1,0:T(8,128)(2,1)}, u32[]{:S(2)}, u32[]{:S(2)}) collective-permute-start(bf16[2,360,1440]{2,1,0:T(8,128)(2,1)} %param.11), channel_id=1, source_target_pairs={{8,0},{16,8},{24,16},{9,1},{17,9},{25,17},{10,2},{18,10},{26,18},{... | collective-permute-start | bytes 6220808 | tf_op jit(solution)/shard_map/ppermute | solution.py:15
  64.8 46.7 %all-reduce = s32[4]{0:T(128)S(1)} all-reduce(s32[4]{0:T(128)S(1)} %dynamic-update-slice), channel_id=1, replica_groups=mesh['grp'=4,'exp'=8] {'grp'}, use_global_device_ids=true, to_apply=%add | all-reduce | flops 4 | bytes 32
  111.5 0.6 convert_reduce_fusion.1
  112.9 3.0 reshape_reshape.3
  115.9 10.4 %fusion.1 = bf16[4,2,360,1440]{3,2,0,1:T(8,128)(2,1)} fusion(f32[]{:T(128)S(6)} %div.13, bf16[8,2,40,4,360]{4,3,2,1,0:T(4,128)(2,1)} %reshape_reshape.3, f32[8,2,40]{2,0,1:T(8,128)S(1)} %copy.56, bf16[8,2,40,1440]{3,2,1,0:T(8,128)(2,1)} %bitcast.17), kind=kOutput, calls=%fused_computation.8 | convolution fusion | flops 2665267200 | bytes 11983364 | tf_op jit(solution)/shard_map/sjmgf,sjmd->gjfd/dot_general | solution.py:82
  126.4 7.8 %copy.67 = bf16[4,2,360,1440]{3,2,1,0:T(8,128)(2,1)} copy(bf16[4,2,360,1440]{3,2,0,1:T(8,128)(2,1)} %fusion.1) | data formatting | bytes 16588800 | tf_op jit(solution)/shard_map/convert_element_type | solution.py:90
  134.2 4.6 %dynamic-slice_bitcast_fusion.2 = (bf16[720,1440]{1,0:T(8,128)(2,1)}, bf16[720,1440]{1,0:T(8,128)(2,1)}) fusion(bf16[4,720,1440]{2,1,0:T(8,128)(2,1)} %bitcast.97, s32[]{:T(128)S(6)} %select_n.61, s32[]{:T(128)S(6)} %max.11), kind=kLoop, calls=%fused_computation.33 | loop fusion | bytes 8294408 | tf_op jit(solution)/shard_map/squeeze | solution.py:29
  138.8 2.0 collective-permute-start.6
  140.9 1.3 collective-permute-start.1
  142.2 9.6 %collective-permute-start.9 = (bf16[720,1440]{1,0:T(8,128)(2,1)}, bf16[720,1440]{1,0:T(8,128)(2,1)}, u32[]{:S(2)}, u32[]{:S(2)}) collective-permute-start(bf16[720,1440]{1,0:T(8,128)(2,1)} %get-tuple-element.18), channel_id=1, source_target_pairs={{24,16},{25,17},{26,18},{27,19},{28,20},{29,21},{30,22},{31,23}} | collective-permute-start | bytes 6220808 | tf_op jit(solution)/shard_map/ppermute | solution.py:32
  151.7 2.1 collective-permute-start.4
  153.8 4.2 %fusion.4 = bf16[720,1440]{1,0:T(8,128)(2,1)} fusion(bf16[720,1440]{1,0:T(8,128)(2,1)} %collective-permute-done.6, bf16[4,720,1440]{2,1,0:T(8,128)(2,1)} %bitcast.98, s32[]{:T(128)S(6)} %select_n.60), kind=kLoop, calls=%fused_computation.15 | loop fusion | flops 4147200 | bytes 6220804 | tf_op jit(solution)/shard_map/convert_element_type | solution.py:29
  158.0 2.0 collective-permute-start.7
  160.1 35.3 %collective-permute-done.1 = bf16[2,360,1440]{2,1,0:T(8,128)(2,1)} collective-permute-done((bf16[2,360,1440]{2,1,0:T(8,128)(2,1)}, bf16[2,360,1440]{2,1,0:T(8,128)(2,1)}, u32[]{:S(2)}, u32[]{:S(2)}) %collective-permute-start.1) | collective-permute-done | bytes 2073632 | tf_op jit(solution)/shard_map/ppermute | solution.py:14
  195.4 1.3 collective-permute-start.2
  196.7 0.8 collective-permute-start.5
  197.5 6.9 %fusion.5 = (bf16[720,1440]{1,0:T(8,128)(2,1)}, bf16[720,1440]{1,0:T(8,128)(2,1)}) fusion(bf16[720,1440]{1,0:T(8,128)(2,1)} %collective-permute-done.7, bf16[4,720,1440]{2,1,0:T(8,128)(2,1)} %bitcast.99, s32[]{:T(128)S(6)} %select_n.59, bf16[720,1440]{1,0:T(8,128)(2,1)} %collective-permute-done.9, s32[]{:T(128)S(6)} %max.10), kind=kLoop, calls=%fused_computation.17 | loop fusion | flops 8294400 | bytes 12441608 | tf_op jit(solution)/shard_map/convert_element_type | solution.py:29
  204.5 52.7 %collective-permute-start.10 = (bf16[720,1440]{1,0:T(8,128)(2,1)}, bf16[720,1440]{1,0:T(8,128)(2,1)}, u32[]{:S(2)}, u32[]{:S(2)}) collective-permute-start(bf16[720,1440]{1,0:T(8,128)(2,1)} %get-tuple-element.16), channel_id=1, source_target_pairs={{16,8},{24,16},{17,9},{25,17},{18,10},{26,18},{19,11},{27,19},{20,... | collective-permute-start | bytes 6220808 | tf_op jit(solution)/shard_map/ppermute | solution.py:32
  257.1 1.5 collective-permute-start.8
  258.7 3.2 bitcast_dynamic-update-slice_fusion.6
  261.8 3.1 bitcast_dynamic-update-slice_fusion.5
  264.9 3.3 bitcast_dynamic-update-slice_fusion.4
  268.2 1.6 bitcast_dynamic-update-slice_fusion.3
  269.8 3.2 bitcast_dynamic-update-slice_fusion.2
  273.0 3.2 bitcast_dynamic-update-slice_fusion.1
  276.2 1.5 bitcast_dynamic-update-slice_fusion
  277.7 7.5 %dynamic-slice_bitcast_fusion = bf16[2,4,360,1440]{3,2,0,1:T(8,128)(2,1)} fusion(bf16[7,2,360,1440]{3,2,1,0:T(8,128)(2,1)} %bitcast_dynamic-update-slice_fusion, s32[]{:T(128)S(6)} %select_n.55), kind=kLoop, calls=%fused_computation.9 | loop fusion | bytes 16588804 | tf_op jit(solution)/shard_map/transpose | solution.py:75
  285.1 7.7 %copy.57 = bf16[2,4,360,1440]{3,2,1,0:T(8,128)(2,1)} copy(bf16[2,4,360,1440]{3,2,0,1:T(8,128)(2,1)} %dynamic-slice_bitcast_fusion) | data formatting | bytes 16588800 | tf_op jit(solution)/shard_map/transpose | solution.py:75
  292.8 7.8 %collective-permute-done.10 = bf16[720,1440]{1,0:T(8,128)(2,1)} collective-permute-done((bf16[720,1440]{1,0:T(8,128)(2,1)}, bf16[720,1440]{1,0:T(8,128)(2,1)}, u32[]{:S(2)}, u32[]{:S(2)}) %collective-permute-start.10) | collective-permute-done | bytes 2073632 | tf_op jit(solution)/shard_map/ppermute | solution.py:32
  300.7 4.2 %fusion.3 = bf16[720,1440]{1,0:T(8,128)(2,1)} fusion(bf16[720,1440]{1,0:T(8,128)(2,1)} %collective-permute-done.10, bf16[4,720,1440]{2,1,0:T(8,128)(2,1)} %bitcast.100, s32[]{:T(128)S(6)} %max.9), kind=kLoop, calls=%fused_computation.13 | loop fusion | flops 4147200 | bytes 6220804 | tf_op jit(solution)/shard_map/convert_element_type | solution.py:30
  304.9 5.8 %collective-permute-start.11 = (bf16[720,1440]{1,0:T(8,128)(2,1)}, bf16[720,1440]{1,0:T(8,128)(2,1)}, u32[]{:S(2)}, u32[]{:S(2)}) collective-permute-start(bf16[720,1440]{1,0:T(8,128)(2,1)} %fusion.3), channel_id=1, source_target_pairs={{8,0},{16,8},{24,16},{9,1},{17,9},{25,17},{10,2},{18,10},{26,18},{... | collective-permute-start | bytes 6220808 | tf_op jit(solution)/shard_map/ppermute | solution.py:32
  310.7 8.7 %fusion.8 = (bf16[8,2,40]{2,0,1:T(8,128)(2,1)S(1)}, bf16[8,2,40,1440]{3,2,0,1:T(8,128)(2,1)}) fusion(f32[8,2,40]{2,0,1:T(8,128)S(1)} %copy.56, bf16[2,1440,1440,1]{2,1,3,0:T(8,128)(2,1)} %bitcast.102, bf16[8,2,40,1440]{3,2,1,0:T(8,128)(2,1)} %bitcast.17, bf16[8,2,40,1440]{3,2,1,0:T(8,128)(2,1)S(1)} %bitcast.103), kind=kOutput, calls=%fused_computation.23 | convolution fusion | flops 2658815488 | bytes 13827840 | tf_op jit(solution)/shard_map/sjmd,jfd->sjmf/dot_general | solution.py:72
  319.4 0.7 convert_element_type.192
  320.1 3.3 all-to-all-start.4
  323.4 3.0 copy.60
  326.4 1.5 all-to-all-done.4
  327.9 3.6 all-to-all-start.2
  331.6 3.5 gather_fusion.1
  335.4 0.7 copy.69
  336.0 20.7 %all-to-all-done.2 = bf16[8,80,1440]{2,1,0:T(8,128)(2,1)S(1)} async-done(((bf16[8,80,1440]{2,1,0:T(8,128)(2,1)}), bf16[8,80,1440]{2,1,0:T(8,128)(2,1)S(1)}, u32[]{:S(2)}, u32[]{:S(2)}) %all-to-all-start.2) | async-done | bytes 1843232 | tf_op jit(solution)/shard_map/all_to_all | solution.py:93
  356.7 2.1 gather_fusion
  358.8 0.4 reshape.189
  359.3 2.4 copy.68
  361.7 5.8 %fusion.6 = f32[720,1440]{1,0:T(8,128)} fusion(bf16[720,1440]{1,0:T(8,128)(2,1)} %collective-permute-done.11, bf16[720,1440]{1,0:T(8,128)(2,1)} %collective-permute-done.8, bf16[4,720,1440]{2,1,0:T(8,128)(2,1)} %bitcast.101, s32[]{:T(128)S(6)} %select_n.58), kind=kLoop, calls=%fused_computation.19 | loop fusion | flops 5184000 | bytes 10368004 | tf_op jit(solution)/shard_map/add | solution.py:34
  (40 shorter events, 1.2 us)
Async XLA Ops:
  10.2 11.9 %all-to-all-start = ((bf16[8,1,80]{2,1,0:T(2,128)(2,1)}), bf16[8,1,80]{2,1,0:T(2,128)(2,1)S(1)}, u32[]{:S(2)}, u32[]{:S(2)}) async-start(bf16[8,1,80]{2,1,0:T(2,128)(2,1)} %all_to_all.25), calls=%async_computation | async-start | bytes 8192 | tf_op jit(solution)/shard_map/all_to_all | solution.py:66
  22.0 4.5 %copy-start.1 = (bf16[128,1440]{0,1:T(8,128)(2,1)S(1)}, bf16[128,1440]{0,1:T(8,128)(2,1)}, u32[]{:S(2)}) copy-start(bf16[128,1440]{0,1:T(8,128)(2,1)} %param.6) | copy-start | bytes 1105924
  22.0 29.7 %all-to-all-start.3 = ((bf16[8,80,1440]{2,1,0:T(8,128)(2,1)}), bf16[8,80,1440]{2,1,0:T(8,128)(2,1)S(1)}, u32[]{:S(2)}, u32[]{:S(2)}) async-start(bf16[8,80,1440]{2,1,0:T(8,128)(2,1)} %bitcast.106), calls=%async_computation.3 | async-start | bytes 3932160 | tf_op jit(solution)/shard_map/all_to_all | solution.py:68
  36.3 21.1 %copy-start.2 = (u32[32]{0:T(128)S(1)}, u32[32]{0:T(128)}, u32[]{:S(2)}) copy-start(u32[32]{0:T(128)} %constant.74) | copy-start | bytes 388
  51.8 64.2 %all-to-all-start.1 = ((bf16[8,80,1440]{2,1,0:T(8,128)(2,1)}), bf16[8,80,1440]{2,1,0:T(8,128)(2,1)}, u32[]{:S(2)}, u32[]{:S(2)}) async-start(bf16[8,80,1440]{2,1,0:T(8,128)(2,1)} %bitcast.104), calls=%async_computation.1 | async-start | bytes 3932160 | tf_op jit(solution)/shard_map/all_to_all | solution.py:65
  56.1 84.8 %collective-permute-start = (bf16[2,360,1440]{2,1,0:T(8,128)(2,1)}, bf16[2,360,1440]{2,1,0:T(8,128)(2,1)}, u32[]{:S(2)}, u32[]{:S(2)}) collective-permute-start(bf16[2,360,1440]{2,1,0:T(8,128)(2,1)} %param.11), channel_id=1, source_target_pairs={{0,8},{8,16},{16,24},{1,9},{9,17},{17,25},{2,10},{10,18},{18,26},{... | collective-permute-start | bytes 6220808 | tf_op jit(solution)/shard_map/ppermute | solution.py:14
  58.8 93.0 %collective-permute-start.3 = (bf16[2,360,1440]{2,1,0:T(8,128)(2,1)}, bf16[2,360,1440]{2,1,0:T(8,128)(2,1)}, u32[]{:S(2)}, u32[]{:S(2)}) collective-permute-start(bf16[2,360,1440]{2,1,0:T(8,128)(2,1)} %param.11), channel_id=1, source_target_pairs={{8,0},{16,8},{24,16},{9,1},{17,9},{25,17},{10,2},{18,10},{26,18},{... | collective-permute-start | bytes 6220808 | tf_op jit(solution)/shard_map/ppermute | solution.py:15
  138.8 15.0 %collective-permute-start.6 = (bf16[720,1440]{1,0:T(8,128)(2,1)}, bf16[720,1440]{1,0:T(8,128)(2,1)}, u32[]{:S(2)}, u32[]{:S(2)}) collective-permute-start(bf16[720,1440]{1,0:T(8,128)(2,1)} %get-tuple-element.17), channel_id=1, source_target_pairs={{0,8},{1,9},{2,10},{3,11},{4,12},{5,13},{6,14},{7,15}} | collective-permute-start | bytes 6220808 | tf_op jit(solution)/shard_map/ppermute | solution.py:31
  140.9 54.6 %collective-permute-start.1 = (bf16[2,360,1440]{2,1,0:T(8,128)(2,1)}, bf16[2,360,1440]{2,1,0:T(8,128)(2,1)}, u32[]{:S(2)}, u32[]{:S(2)}) collective-permute-start(bf16[2,360,1440]{2,1,0:T(8,128)(2,1)} %collective-permute-done), channel_id=1, source_target_pairs={{8,16},{16,24},{9,17},{17,25},{10,18},{18,26},{11,19},{19,27},{12,... | collective-permute-start | bytes 6220808 | tf_op jit(solution)/shard_map/ppermute | solution.py:14
  142.2 55.4 %collective-permute-start.9 = (bf16[720,1440]{1,0:T(8,128)(2,1)}, bf16[720,1440]{1,0:T(8,128)(2,1)}, u32[]{:S(2)}, u32[]{:S(2)}) collective-permute-start(bf16[720,1440]{1,0:T(8,128)(2,1)} %get-tuple-element.18), channel_id=1, source_target_pairs={{24,16},{25,17},{26,18},{27,19},{28,20},{29,21},{30,22},{31,23}} | collective-permute-start | bytes 6220808 | tf_op jit(solution)/shard_map/ppermute | solution.py:32
  151.7 45.0 %collective-permute-start.4 = (bf16[2,360,1440]{2,1,0:T(8,128)(2,1)}, bf16[2,360,1440]{2,1,0:T(8,128)(2,1)}, u32[]{:S(2)}, u32[]{:S(2)}) collective-permute-start(bf16[2,360,1440]{2,1,0:T(8,128)(2,1)} %collective-permute-done.3), channel_id=1, source_target_pairs={{8,0},{16,8},{9,1},{17,9},{10,2},{18,10},{11,3},{19,11},{12,4},{20... | collective-permute-start | bytes 6220808 | tf_op jit(solution)/shard_map/ppermute | solution.py:15
  158.0 39.5 %collective-permute-start.7 = (bf16[720,1440]{1,0:T(8,128)(2,1)}, bf16[720,1440]{1,0:T(8,128)(2,1)}, u32[]{:S(2)}, u32[]{:S(2)}) collective-permute-start(bf16[720,1440]{1,0:T(8,128)(2,1)} %fusion.4), channel_id=1, source_target_pairs={{0,8},{8,16},{1,9},{9,17},{2,10},{10,18},{3,11},{11,19},{4,12},{12... | collective-permute-start | bytes 6220808 | tf_op jit(solution)/shard_map/ppermute | solution.py:31
  195.4 63.2 %collective-permute-start.2 = (bf16[2,360,1440]{2,1,0:T(8,128)(2,1)}, bf16[2,360,1440]{2,1,0:T(8,128)(2,1)}, u32[]{:S(2)}, u32[]{:S(2)}) collective-permute-start(bf16[2,360,1440]{2,1,0:T(8,128)(2,1)} %collective-permute-done.1), channel_id=1, source_target_pairs={{16,24},{17,25},{18,26},{19,27},{20,28},{21,29},{22,30},{23,31}} | collective-permute-start | bytes 6220808 | tf_op jit(solution)/shard_map/ppermute | solution.py:14
  196.7 79.5 %collective-permute-start.5 = (bf16[2,360,1440]{2,1,0:T(8,128)(2,1)}, bf16[2,360,1440]{2,1,0:T(8,128)(2,1)S(1)}, u32[]{:S(2)}, u32[]{:S(2)}) collective-permute-start(bf16[2,360,1440]{2,1,0:T(8,128)(2,1)} %collective-permute-done.4), channel_id=1, source_target_pairs={{8,0},{9,1},{10,2},{11,3},{12,4},{13,5},{14,6},{15,7}} | collective-permute-start | bytes 6220808 | tf_op jit(solution)/shard_map/ppermute | solution.py:15
  204.5 96.2 %collective-permute-start.10 = (bf16[720,1440]{1,0:T(8,128)(2,1)}, bf16[720,1440]{1,0:T(8,128)(2,1)}, u32[]{:S(2)}, u32[]{:S(2)}) collective-permute-start(bf16[720,1440]{1,0:T(8,128)(2,1)} %get-tuple-element.16), channel_id=1, source_target_pairs={{16,8},{24,16},{17,9},{25,17},{18,10},{26,18},{19,11},{27,19},{20,... | collective-permute-start | bytes 6220808 | tf_op jit(solution)/shard_map/ppermute | solution.py:32
  257.1 104.6 %collective-permute-start.8 = (bf16[720,1440]{1,0:T(8,128)(2,1)}, bf16[720,1440]{1,0:T(8,128)(2,1)}, u32[]{:S(2)}, u32[]{:S(2)}) collective-permute-start(bf16[720,1440]{1,0:T(8,128)(2,1)} %get-tuple-element.15), channel_id=1, source_target_pairs={{0,8},{8,16},{16,24},{1,9},{9,17},{17,25},{2,10},{10,18},{18,26},{... | collective-permute-start | bytes 6220808 | tf_op jit(solution)/shard_map/ppermute | solution.py:31
  264.9 3.3 copy-start
  304.9 56.8 %collective-permute-start.11 = (bf16[720,1440]{1,0:T(8,128)(2,1)}, bf16[720,1440]{1,0:T(8,128)(2,1)}, u32[]{:S(2)}, u32[]{:S(2)}) collective-permute-start(bf16[720,1440]{1,0:T(8,128)(2,1)} %fusion.3), channel_id=1, source_target_pairs={{8,0},{16,8},{24,16},{9,1},{17,9},{25,17},{10,2},{18,10},{26,18},{... | collective-permute-start | bytes 6220808 | tf_op jit(solution)/shard_map/ppermute | solution.py:32
  320.1 7.8 %all-to-all-start.4 = ((bf16[8,1,80]{2,1,0:T(2,128)(2,1)}), bf16[8,1,80]{2,1,0:T(2,128)(2,1)S(1)}, u32[]{:S(2)}, u32[]{:S(2)}) async-start(bf16[8,1,80]{2,1,0:T(2,128)(2,1)} %convert_element_type.192), calls=%async_computation.4 | async-start | bytes 8192 | tf_op jit(solution)/shard_map/all_to_all | solution.py:100
  327.9 28.8 %all-to-all-start.2 = ((bf16[8,80,1440]{2,1,0:T(8,128)(2,1)}), bf16[8,80,1440]{2,1,0:T(8,128)(2,1)S(1)}, u32[]{:S(2)}, u32[]{:S(2)}) async-start(bf16[8,80,1440]{2,1,0:T(8,128)(2,1)} %bitcast.105), calls=%async_computation.2 | async-start | bytes 3932160 | tf_op jit(solution)/shard_map/all_to_all | solution.py:93

commit v5 on v3

--- a/solution.py
+++ b/solution.py
@@ -56,12 +56,9 @@
     dy_four = dy_recv.reshape(n_exp, exp_dev, most, width)
     hid_four = hid_recv.reshape(n_exp, exp_dev, most, ffw)
     gate_three = gate_recv.reshape(n_exp, exp_dev, most).astype(jnp.float32)
-    proj = jnp.einsum(
-        "sjmd,jfd->sjmf",
-        dy_four,
-        lax.all_gather(w_down, "grp", axis=1, tiled=True),
-        preferred_element_type=jnp.float32,
-    )
+    w_full = lax.all_gather(w_down, "grp", axis=1, tiled=True)
+    proj = jnp.einsum("sjmd,jfd->sjmf", dy_four, w_full, preferred_element_type=jnp.float32)
+    after_gather = jnp.abs(w_full[0, 0, 0]) < jnp.inf
     dh_rows = (gate_three[..., None] * proj).astype(jnp.bfloat16)
     inner = jnp.sum(hid_four.astype(jnp.float32) * proj, axis=3).astype(jnp.bfloat16)
     scaled = (gate_three[..., None] * dy_four.astype(jnp.float32)).astype(jnp.bfloat16)
@@ -74,7 +71,8 @@
         )
         * scale
     )
-    grad_parts = partial_grad.astype(jnp.bfloat16).reshape(n_grp, exp_dev * (ffw // n_grp), width)
+    grad_parts = jnp.where(after_gather, partial_grad, 0.0).astype(jnp.bfloat16)
+    grad_parts = grad_parts.reshape(n_grp, exp_dev * (ffw // n_grp), width)
     d_weight = line_reduce_scatter(grad_parts, n_grp).reshape(exp_dev, ffw // n_grp, width)
     back_dh, back_inner = (
         lax.all_to_all(

time: 422 us -> 429 us (1.017); the launches traced: 422 us -> 424 us
  waiting for transfers between devices: 254 us -> 260 us
    all_gather x1, waiting for transfers between devices: 0.02 us -> 93.4 us  [body(): w_full = lax.all_gather(w_down, 'grp', axis=1, tiled=True)]
    ppermute x3, waiting for transfers between devices: 176 us -> 90.6 us  [line_reduce_scatter(): right = lax.ppermute(send_r, 'grp', [(g, g + 1) for g in range(k)])]
    all_to_all x1, waiting for transfers between devices: 0.01 us -> 19.3 us  [body(): lax.all_to_all(dh_rows.reshape(n_exp, exp_dev * most, ffw), 'exp', split_...]
    ppermute x3, waiting for transfers between devices: 54.5 us -> 42.3 us  [line_reduce_scatter(): left = lax.ppermute(send_l, 'grp', [(g, g - 1) for g in range(n - k, n)])]
    all_to_all x1, waiting for transfers between devices: 9.5 us -> 0.01 us  [body(): lax.all_to_all(dy_buf, 'exp', split_axis=0, concat_axis=0, tiled=True)]
  transfers between devices with their start and end apart: 12 -> 12, of which waited for: 7 -> 7; matrix products, arithmetic and copies ran while one was open for 20% -> 14% of each run, Pallas kernels for 0% -> 0%
where the time goes in v5:
time: 429 us; the launch traced here: 424 us
  waiting for transfers between devices  260 us (61%)
  local copies, waits for them, and re-layouts  53.3 us (12%)
  starting transfers between devices  42.7 us (10%)
  other arithmetic  23.3 us (5%)
  matrix products  19.4 us (5%)
  between operations  16.3 us (4%)
  blocking collectives  8.61 us (2%)
    all_gather x1, waiting for transfers between devices, body(): w_full = lax.all_gather(w_down, 'grp', axis=1, tiled=True)  93.4 us
    ppermute x3, waiting for transfers between devices, line_reduce_scatter(): right = lax.ppermute(send_r, 'grp', [(g, g + 1) for g in range(k)])  90.6 us
    ppermute x3, waiting for transfers between devices, line_reduce_scatter(): left = lax.ppermute(send_l, 'grp', [(g, g - 1) for g in range(n - k, n)])  42.3 us
    all_to_all x1, waiting for transfers between devices, body(): lax.all_to_all(dh_rows.reshape(n_exp, exp_dev * most, ffw), 'exp', split_...  19.3 us
    all_to_all x1, waiting for transfers between devices, body(): lax.all_to_all(hid_buf, 'exp', split_axis=0, concat_axis=0, tiled=True)  14 us
    ppermute x3, starting transfers between devices, line_reduce_scatter(): right = lax.ppermute(send_r, 'grp', [(g, g + 1) for g in range(k)])  13.5 us
    convert_element_type x2, other arithmetic, line_reduce_scatter(): (parts[s_r].astype(jnp.float32) + right.astype(jnp.float32)).astype(parts...  11.1 us
    dot_general x1, matrix products, body(): jnp.einsum('sjmgf,sjmd->gjfd', hid_four.reshape(n_exp, exp_dev, most, n_g...  10.6 us
  transfers between devices with their start and end apart: 12, of which 7 were waited for; matrix products, arithmetic and copies ran while one was open for 14% of the time, Pallas kernels for 0%

profile of v5, /device:TPU:2, one launch (start us, length us, event | category | flops | bytes accessed | tf_op | source)
XLA Modules:
  0.0 423.8 jit_solution(6322184172124024441)
XLA Ops:
  7.2 0.0 all-gather.2.cloned.1.call-start
  7.2 0.7 all-gather.2.cloned.1.call-update
  7.9 0.1 copy.47
  8.1 0.1 eq.25
  8.2 0.1 eq.29
  8.3 0.1 copy.46
  8.4 0.1 mul.62
  8.5 1.2 reduce-window.6
  9.7 0.2 slice_reduce_fusion
  10.6 0.1 copy.51
  10.8 0.1 reshape.230
  10.9 0.1 fusion.25
  11.0 3.8 scatter_custom_fusion
  14.8 0.7 all_to_all.25
  15.5 4.3 %all-to-all-start = ((bf16[8,1,80]{2,1,0:T(2,128)(2,1)}), bf16[8,1,80]{2,1,0:T(2,128)(2,1)S(1)}, u32[]{:S(2)}, u32[]{:S(2)}) async-start(bf16[8,1,80]{2,1,0:T(2,128)(2,1)} %all_to_all.25), calls=%async_computation | async-start | bytes 8192 | tf_op jit(solution)/shard_map/all_to_all | solution.py:53
  19.7 1.6 copy.57
  21.3 0.8 reshape.246
  22.1 4.5 %scatter_custom_fusion.2 = bf16[640,1440]{1,0:T(8,128)(2,1)} fusion(s32[512]{0:T(512)S(1)} %bitcast.96, bf16[512,1440]{1,0:T(8,128)(2,1)S(1)} %reshape.246, bf16[]{:T(256)} %constant.53.clone.1), kind=kCustom, calls=%fused_computation.36 | custom fusion | bytes 1843202 | tf_op jit(solution)/shard_map/scatter | solution.py:46
  26.6 0.0 all-to-all-done
  26.6 4.3 %all-to-all-start.3 = ((bf16[8,80,1440]{2,1,0:T(8,128)(2,1)}), bf16[8,80,1440]{2,1,0:T(8,128)(2,1)S(1)}, u32[]{:S(2)}, u32[]{:S(2)}) async-start(bf16[8,80,1440]{2,1,0:T(8,128)(2,1)} %bitcast.93), calls=%async_computation.3 | async-start | bytes 3932160 | tf_op jit(solution)/shard_map/all_to_all | solution.py:55
  30.9 0.2 copy.54
  31.1 9.6 %scatter_custom_fusion.1 = bf16[640,1440]{1,0:T(8,128)(2,1)} fusion(s32[512]{0:T(512)S(1)} %bitcast.97, bf16[128,1440]{1,0:T(8,128)(2,1)S(1)} %copy.54, s32[1024]{0:T(1024)S(1)} %pad_clamp_fusion.1, bf16[]{:T(256)} %constant.53.clone.1), kind=kCustom, calls=%fused_computation.34 | custom fusion | bytes 1843202 | tf_op jit(solution)/shard_map/scatter | solution.py:45
  40.7 14.0 %all-to-all-done.3 = bf16[8,80,1440]{2,1,0:T(8,128)(2,1)S(1)} async-done(((bf16[8,80,1440]{2,1,0:T(8,128)(2,1)}), bf16[8,80,1440]{2,1,0:T(8,128)(2,1)S(1)}, u32[]{:S(2)}, u32[]{:S(2)}) %all-to-all-start.3) | async-done | bytes 1843232 | tf_op jit(solution)/shard_map/all_to_all | solution.py:55
  54.7 5.7 %all-to-all-start.1 = ((bf16[8,80,1440]{2,1,0:T(8,128)(2,1)}), bf16[8,80,1440]{2,1,0:T(8,128)(2,1)}, u32[]{:S(2)}, u32[]{:S(2)}) async-start(bf16[8,80,1440]{2,1,0:T(8,128)(2,1)} %bitcast.91), calls=%async_computation.1 | async-start | bytes 3932160 | tf_op jit(solution)/shard_map/all_to_all | solution.py:52
  60.4 0.6 dynamic-slice
  61.0 0.8 dynamic-update-slice
  61.8 8.6 %all-reduce = s32[4]{0:T(128)S(1)} all-reduce(s32[4]{0:T(128)S(1)} %dynamic-update-slice), channel_id=1, replica_groups=mesh['grp'=4,'exp'=8] {'grp'}, use_global_device_ids=true, to_apply=%add | all-reduce | flops 4 | bytes 32
  70.4 0.6 convert_reduce_fusion.1
  71.7 0.1 reshape.194
  71.8 3.0 reshape_reshape.3
  74.8 93.4 %all-gather.2.cloned.1.call-done = bf16[2,1440,1440]{2,1,0:T(8,128)(2,1)} async-done(((bf16[2,360,1440]{2,1,0:T(8,128)(2,1)}), bf16[2,1440,1440]{2,1,0:T(8,128)(2,1)}) %all-gather.2.cloned.1.call-update) | async-done | bytes 8294416 | tf_op jit(solution)/shard_map/all_gather | solution.py:59
  168.2 1.2 slice.19
  170.0 10.6 %fusion.2 = bf16[4,2,360,1440]{3,2,0,1:T(8,128)(2,1)} fusion(f32[]{:T(128)S(6)} %div.13, pred[]{:T(512)} %bitcast.14, bf16[8,2,40,4,360]{4,3,2,1,0:T(4,128)(2,1)} %reshape_reshape.3, f32[8,2,40]{2,0,1:T(8,128)S(1)} %copy.53, bf16[8,2,40,1440]{3,2,1,0:T(8,128)(2,1)} %bitcast.6), kind=kOutput, calls=%fused_computation.9 | convolution fusion | flops 2669414400 | bytes 11983365 | tf_op jit(solution)/shard_map/sjmgf,sjmd->gjfd/dot_general | solution.py:66
  180.6 7.8 %copy.63 = bf16[4,2,360,1440]{3,2,1,0:T(8,128)(2,1)} copy(bf16[4,2,360,1440]{3,2,0,1:T(8,128)(2,1)} %fusion.2) | data formatting | bytes 16588800 | tf_op jit(solution)/shard_map/convert_element_type | solution.py:74
  188.4 4.7 %dynamic-slice_bitcast_fusion.1 = (bf16[720,1440]{1,0:T(8,128)(2,1)}, bf16[720,1440]{1,0:T(8,128)(2,1)}) fusion(bf16[4,720,1440]{2,1,0:T(8,128)(2,1)} %bitcast.85, s32[]{:T(128)S(6)} %select_n.68, s32[]{:T(128)S(6)} %max.11), kind=kLoop, calls=%fused_computation.28 | loop fusion | bytes 8294408 | tf_op jit(solution)/shard_map/squeeze | solution.py:16
  193.1 2.7 collective-permute-start
  195.8 2.0 collective-permute-start.3
  197.8 44.7 %collective-permute-done = bf16[720,1440]{1,0:T(8,128)(2,1)} collective-permute-done((bf16[720,1440]{1,0:T(8,128)(2,1)}, bf16[720,1440]{1,0:T(8,128)(2,1)}, u32[]{:S(2)}, u32[]{:S(2)}) %collective-permute-start) | collective-permute-done | bytes 2073632 | tf_op jit(solution)/shard_map/ppermute | solution.py:18
  242.6 4.2 fusion.7
  246.8 5.8 %collective-permute-start.1 = (bf16[720,1440]{1,0:T(8,128)(2,1)}, bf16[720,1440]{1,0:T(8,128)(2,1)}, u32[]{:S(2)}, u32[]{:S(2)}) collective-permute-start(bf16[720,1440]{1,0:T(8,128)(2,1)} %fusion.7), channel_id=1, source_target_pairs={{0,8},{8,16},{1,9},{9,17},{2,10},{10,18},{3,11},{11,19},{4,12},{12... | collective-permute-start | bytes 6220808 | tf_op jit(solution)/shard_map/ppermute | solution.py:18
  252.6 0.0 collective-permute-done.3
  252.6 45.9 %collective-permute-done.1 = bf16[720,1440]{1,0:T(8,128)(2,1)} collective-permute-done((bf16[720,1440]{1,0:T(8,128)(2,1)}, bf16[720,1440]{1,0:T(8,128)(2,1)}, u32[]{:S(2)}, u32[]{:S(2)}) %collective-permute-start.1) | collective-permute-done | bytes 2073632 | tf_op jit(solution)/shard_map/ppermute | solution.py:18
  298.5 6.9 %fusion.8 = (bf16[720,1440]{1,0:T(8,128)(2,1)}, bf16[720,1440]{1,0:T(8,128)(2,1)}) fusion(bf16[720,1440]{1,0:T(8,128)(2,1)} %collective-permute-done.1, bf16[4,720,1440]{2,1,0:T(8,128)(2,1)} %bitcast.87, s32[]{:T(128)S(6)} %select_n.66, bf16[720,1440]{1,0:T(8,128)(2,1)} %collective-permute-done.3, s32[]{:T(128)S(6)} %max.10), kind=kLoop, calls=%fused_computation.19 | loop fusion | flops 8294400 | bytes 12441608 | tf_op jit(solution)/shard_map/convert_element_type | solution.py:16
  305.4 2.0 collective-permute-start.4
  307.4 5.0 %collective-permute-start.2 = (bf16[720,1440]{1,0:T(8,128)(2,1)}, bf16[720,1440]{1,0:T(8,128)(2,1)}, u32[]{:S(2)}, u32[]{:S(2)}) collective-permute-start(bf16[720,1440]{1,0:T(8,128)(2,1)} %get-tuple-element.15), channel_id=1, source_target_pairs={{0,8},{8,16},{16,24},{1,9},{9,17},{17,25},{2,10},{10,18},{18,26},{... | collective-permute-start | bytes 6220808 | tf_op jit(solution)/shard_map/ppermute | solution.py:18
  312.5 4.3 %fusion.6 = bf16[720,1440]{1,0:T(8,128)(2,1)} fusion(bf16[720,1440]{1,0:T(8,128)(2,1)} %collective-permute-done.4, bf16[4,720,1440]{2,1,0:T(8,128)(2,1)} %bitcast.88, s32[]{:T(128)S(6)} %max.9), kind=kLoop, calls=%fused_computation.15 | loop fusion | flops 4147200 | bytes 6220804 | tf_op jit(solution)/shard_map/convert_element_type | solution.py:17
  316.8 1.5 collective-permute-start.5
  318.3 8.8 %fusion.11 = (bf16[8,2,40]{2,0,1:T(8,128)(2,1)S(1)}, bf16[8,2,40,1440]{3,2,0,1:T(8,128)(2,1)}) fusion(f32[8,2,40]{2,0,1:T(8,128)S(1)} %copy.53, bf16[2,1440,1440]{2,1,0:T(8,128)(2,1)} %all-gather.2.cloned.1.call-done, bf16[8,2,40,1440]{3,2,1,0:T(8,128)(2,1)} %bitcast.6, bf16[8,2,40,1440]{3,2,1,0:T(8,128)(2,1)S(1)} %bitcast.90), kind=kOutput, calls=%fused_computation.25 | convolution fusion | flops 2658815488 | bytes 13827840 | tf_op jit(solution)/shard_map/sjmd,jfd->sjmf/dot_general | solution.py:60
  327.1 0.7 convert_element_type.192
  327.8 4.2 all-to-all-start.4
  332.0 3.0 copy.56
  335.0 0.1 all-to-all-done.4
  335.1 5.0 %all-to-all-start.2 = ((bf16[8,80,1440]{2,1,0:T(8,128)(2,1)}), bf16[8,80,1440]{2,1,0:T(8,128)(2,1)S(1)}, u32[]{:S(2)}, u32[]{:S(2)}) async-start(bf16[8,80,1440]{2,1,0:T(8,128)(2,1)} %bitcast.92), calls=%async_computation.2 | async-start | bytes 3932160 | tf_op jit(solution)/shard_map/all_to_all | solution.py:78
  340.1 0.1 reshape.191
  340.2 3.5 gather_fusion.1
  343.8 0.1 reshape.196
  343.9 0.1 multiply_convert_fusion.1
  344.0 0.7 copy.65
  344.6 19.3 %all-to-all-done.2 = bf16[8,80,1440]{2,1,0:T(8,128)(2,1)S(1)} async-done(((bf16[8,80,1440]{2,1,0:T(8,128)(2,1)}), bf16[8,80,1440]{2,1,0:T(8,128)(2,1)S(1)}, u32[]{:S(2)}, u32[]{:S(2)}) %all-to-all-start.2) | async-done | bytes 1843232 | tf_op jit(solution)/shard_map/all_to_all | solution.py:78
  363.9 2.1 gather_fusion
  366.0 0.4 reshape.188
  366.4 2.4 copy.64
  368.9 42.3 %collective-permute-done.5 = bf16[720,1440]{1,0:T(8,128)(2,1)} collective-permute-done((bf16[720,1440]{1,0:T(8,128)(2,1)}, bf16[720,1440]{1,0:T(8,128)(2,1)}, u32[]{:S(2)}, u32[]{:S(2)}) %collective-permute-start.5) | collective-permute-done | bytes 2073632 | tf_op jit(solution)/shard_map/ppermute | solution.py:19
  411.1 5.8 %fusion.9 = f32[720,1440]{1,0:T(8,128)} fusion(bf16[720,1440]{1,0:T(8,128)(2,1)} %collective-permute-done.5, bf16[720,1440]{1,0:T(8,128)(2,1)} %collective-permute-done.2, bf16[4,720,1440]{2,1,0:T(8,128)(2,1)} %bitcast.89, s32[]{:T(128)S(6)} %select_n.65), kind=kLoop, calls=%fused_computation.21 | loop fusion | flops 5184000 | bytes 10368004 | tf_op jit(solution)/shard_map/add | solution.py:21
  (27 shorter events, 0.2 us)
Async XLA Ops:
  7.2 0.8 copy-start.2
  7.2 3.4 copy-start.3
  7.2 12.5 %copy-start = (bf16[128,4,1440]{0,2,1:T(8,128)(2,1)S(1)}, bf16[128,4,1440]{0,2,1:T(8,128)(2,1)}, u32[]{:S(2)}) copy-start(bf16[128,4,1440]{0,2,1:T(8,128)(2,1)} %param.7) | copy-start | bytes 4423684
  7.2 161.0 %all-gather.2.cloned.1.call-start = ((), (), s32[]{:S(2)}) async-start(), calls=%async_computation.5 | async-start | bytes 11059200 | tf_op jit(solution)/shard_map/all_gather | solution.py:59
  15.5 11.2 %all-to-all-start = ((bf16[8,1,80]{2,1,0:T(2,128)(2,1)}), bf16[8,1,80]{2,1,0:T(2,128)(2,1)S(1)}, u32[]{:S(2)}, u32[]{:S(2)}) async-start(bf16[8,1,80]{2,1,0:T(2,128)(2,1)} %all_to_all.25), calls=%async_computation | async-start | bytes 8192 | tf_op jit(solution)/shard_map/all_to_all | solution.py:53
  26.6 4.3 %copy-start.1 = (bf16[128,1440]{0,1:T(8,128)(2,1)S(1)}, bf16[128,1440]{0,1:T(8,128)(2,1)}, u32[]{:S(2)}) copy-start(bf16[128,1440]{0,1:T(8,128)(2,1)} %param.6) | copy-start | bytes 1105924
  26.6 28.1 %all-to-all-start.3 = ((bf16[8,80,1440]{2,1,0:T(8,128)(2,1)}), bf16[8,80,1440]{2,1,0:T(8,128)(2,1)S(1)}, u32[]{:S(2)}, u32[]{:S(2)}) async-start(bf16[8,80,1440]{2,1,0:T(8,128)(2,1)} %bitcast.93), calls=%async_computation.3 | async-start | bytes 3932160 | tf_op jit(solution)/shard_map/all_to_all | solution.py:55
  40.7 19.7 %copy-start.4 = (u32[32]{0:T(128)S(1)}, u32[32]{0:T(128)}, u32[]{:S(2)}) copy-start(u32[32]{0:T(128)} %constant.74) | copy-start | bytes 388
  54.7 115.4 %all-to-all-start.1 = ((bf16[8,80,1440]{2,1,0:T(8,128)(2,1)}), bf16[8,80,1440]{2,1,0:T(8,128)(2,1)}, u32[]{:S(2)}, u32[]{:S(2)}) async-start(bf16[8,80,1440]{2,1,0:T(8,128)(2,1)} %bitcast.91), calls=%async_computation.1 | async-start | bytes 3932160 | tf_op jit(solution)/shard_map/all_to_all | solution.py:52
  193.1 49.4 %collective-permute-start = (bf16[720,1440]{1,0:T(8,128)(2,1)}, bf16[720,1440]{1,0:T(8,128)(2,1)}, u32[]{:S(2)}, u32[]{:S(2)}) collective-permute-start(bf16[720,1440]{1,0:T(8,128)(2,1)} %get-tuple-element.17), channel_id=1, source_target_pairs={{0,8},{1,9},{2,10},{3,11},{4,12},{5,13},{6,14},{7,15}} | collective-permute-start | bytes 6220808 | tf_op jit(solution)/shard_map/ppermute | solution.py:18
  195.8 56.8 %collective-permute-start.3 = (bf16[720,1440]{1,0:T(8,128)(2,1)}, bf16[720,1440]{1,0:T(8,128)(2,1)}, u32[]{:S(2)}, u32[]{:S(2)}) collective-permute-start(bf16[720,1440]{1,0:T(8,128)(2,1)} %get-tuple-element.18), channel_id=1, source_target_pairs={{24,16},{25,17},{26,18},{27,19},{28,20},{29,21},{30,22},{31,23}} | collective-permute-start | bytes 6220808 | tf_op jit(solution)/shard_map/ppermute | solution.py:19
  246.8 51.7 %collective-permute-start.1 = (bf16[720,1440]{1,0:T(8,128)(2,1)}, bf16[720,1440]{1,0:T(8,128)(2,1)}, u32[]{:S(2)}, u32[]{:S(2)}) collective-permute-start(bf16[720,1440]{1,0:T(8,128)(2,1)} %fusion.7), channel_id=1, source_target_pairs={{0,8},{8,16},{1,9},{9,17},{2,10},{10,18},{3,11},{11,19},{4,12},{12... | collective-permute-start | bytes 6220808 | tf_op jit(solution)/shard_map/ppermute | solution.py:18
  305.4 7.1 %collective-permute-start.4 = (bf16[720,1440]{1,0:T(8,128)(2,1)}, bf16[720,1440]{1,0:T(8,128)(2,1)}, u32[]{:S(2)}, u32[]{:S(2)}) collective-permute-start(bf16[720,1440]{1,0:T(8,128)(2,1)} %get-tuple-element.16), channel_id=1, source_target_pairs={{16,8},{24,16},{17,9},{25,17},{18,10},{26,18},{19,11},{27,19},{20,... | collective-permute-start | bytes 6220808 | tf_op jit(solution)/shard_map/ppermute | solution.py:19
  307.4 61.4 %collective-permute-start.2 = (bf16[720,1440]{1,0:T(8,128)(2,1)}, bf16[720,1440]{1,0:T(8,128)(2,1)}, u32[]{:S(2)}, u32[]{:S(2)}) collective-permute-start(bf16[720,1440]{1,0:T(8,128)(2,1)} %get-tuple-element.15), channel_id=1, source_target_pairs={{0,8},{8,16},{16,24},{1,9},{9,17},{17,25},{2,10},{10,18},{18,26},{... | collective-permute-start | bytes 6220808 | tf_op jit(solution)/shard_map/ppermute | solution.py:18
  316.8 94.4 %collective-permute-start.5 = (bf16[720,1440]{1,0:T(8,128)(2,1)}, bf16[720,1440]{1,0:T(8,128)(2,1)}, u32[]{:S(2)}, u32[]{:S(2)}) collective-permute-start(bf16[720,1440]{1,0:T(8,128)(2,1)} %fusion.6), channel_id=1, source_target_pairs={{8,0},{16,8},{24,16},{9,1},{17,9},{25,17},{10,2},{18,10},{26,18},{... | collective-permute-start | bytes 6220808 | tf_op jit(solution)/shard_map/ppermute | solution.py:19
  327.8 7.3 %all-to-all-start.4 = ((bf16[8,1,80]{2,1,0:T(2,128)(2,1)}), bf16[8,1,80]{2,1,0:T(2,128)(2,1)S(1)}, u32[]{:S(2)}, u32[]{:S(2)}) async-start(bf16[8,1,80]{2,1,0:T(2,128)(2,1)} %convert_element_type.192), calls=%async_computation.4 | async-start | bytes 8192 | tf_op jit(solution)/shard_map/all_to_all | solution.py:85
  335.1 28.7 %all-to-all-start.2 = ((bf16[8,80,1440]{2,1,0:T(8,128)(2,1)}), bf16[8,80,1440]{2,1,0:T(8,128)(2,1)S(1)}, u32[]{:S(2)}, u32[]{:S(2)}) async-start(bf16[8,80,1440]{2,1,0:T(8,128)(2,1)} %bitcast.92), calls=%async_computation.2 | async-start | bytes 3932160 | tf_op jit(solution)/shard_map/all_to_all | solution.py:78
Sparse Core Ops, SparseCore 0:
  9.6 158.5 all-gather.1
